TPU v7x, 32 devices: a whole 2x2x4 slice. The times are simulated.
32 devices in a mesh: lines: 2 (over x), col: 16 (over z, y, core).
Axes of the slice: x: 2, y: 2, z: 4, core: 2. Of those that a mesh axis runs over, the one named last changes fastest.
Arguments:
- primary: float32 [16, 4, 128, 256], P(None, 'lines', 'col'), parts along dimension 1, may hold values from -6 to 6
- conductivity: float32 [128, 512], P('col', 'lines'), parts along dimension 1, may hold values from 0.1 to 10
- wavenumbers: float32 [16], replicated, may hold values from 0.05 to 1.5
- quadrature: float32 [16], replicated, may hold values from 0.02 to 0.2
- electrodes: int32 [64], P(('lines', 'col')), parts along dimension 0, may hold values from 0 to 127, as said below
- far_pole: int32 [4, 32], P('lines'), parts along dimension 0, may hold values from 0 to 31, as said below
- observed: float32 [4, 32], P('lines'), parts along dimension 0, may hold values from -6 to 6
- prior_adjoint: float32 [16, 4, 128, 256], P(None, 'lines', 'col'), parts along dimension 1, may hold values from -0.012 to 0.012
Outputs:
- predicted: float32 [4, 32], P('lines'), parts along dimension 0
- gradient: float32 [128, 512], P('col', 'lines'), parts along dimension 1
There are 2 independent parts, one for each index of `lines`. A program takes and returns all parts, laid end to end along the dimension named above; an argument that names none is the same for every part. Nothing has to cross between parts.
Inputs may be any that keep to these rules, and one draw needn't show every extreme that they name: electrodes[e] lies in columns 4 e to 4 e + 3. far_pole[s, r] differs from r by 1 to 8.
All inputs are finite; a program needn't handle non-finite values.
Results may differ from a plain program's by a relative error of at most 0.0003.
Values sent between devices are 32-bit elements; how exact they have to be, the bound alone decides.
No kernel may reach another device: no remote copies, remote signals or barrier semaphores. Data moves between devices by JAX's collectives and lax.ppermute only.
A program may use at most 64 MiB of HBM per device.

v0:
```python
import jax
import jax.numpy as jnp
from jax import lax
from jax.sharding import PartitionSpec as P

ITERS = 2


def padded_2(block, sides, width):
    for axis, dim in sides:
        count = lax.axis_size(axis)
        forward = [(i, i + 1) for i in range(count - 1)]
        backward = [(target, source) for source, target in forward]
        low = lax.ppermute(
            lax.slice_in_dim(block, block.shape[dim] - width, None, axis=dim), axis, forward
        )
        high = lax.ppermute(lax.slice_in_dim(block, 0, width, axis=dim), axis, backward)
        block = jnp.concatenate([low, block, high], axis=dim)
    return block


def shifted(value, axis, steps):
    count = lax.axis_size(axis)
    initial, last = (max(0, -steps), min(count, count - steps))
    return lax.ppermute(value, axis, [(source, source + steps) for source in range(initial, last)])


def coefficients(sigma_wide):
    center = sigma_wide[1:-1]
    west_face = 0.5 * (center + sigma_wide[:-2])
    east_face = 0.5 * (center + sigma_wide[2:])
    below_sigma = jnp.concatenate([center[:, 1:], jnp.zeros_like(center[:, :1])], axis=1)
    lower_face = 0.5 * (center + below_sigma)
    above_sigma = jnp.concatenate([jnp.zeros_like(center[:, :1]), center[:, :-1]], axis=1)
    upper_face = 0.5 * (center + above_sigma)
    top_row = jnp.arange(center.shape[1]) == 0
    upper_face = jnp.where(top_row[None, :], 0.0, upper_face)
    return (west_face, east_face, lower_face, upper_face, center)


def stencil(field_wide, faces_set, mass_scale):
    west_face, east_face, lower_face, upper_face, center = faces_set
    middle = field_wide[..., 1:-1, :]
    below_cells = jnp.concatenate([middle[..., 1:], jnp.zeros_like(middle[..., :1])], axis=-1)
    above_cells = jnp.concatenate([jnp.zeros_like(middle[..., :1]), middle[..., :-1]], axis=-1)
    result = west_face * (middle - field_wide[..., :-2, :]) + east_face * (
        middle - field_wide[..., 2:, :]
    )
    result = result + lower_face * (middle - below_cells) + upper_face * (middle - above_cells)
    return result + mass_scale * center * middle


def local_sum(left_field, right_field):
    return jnp.sum(left_field * right_field, axis=(2, 3))


def squares(residual):
    return lax.psum(local_sum(residual, residual), "col")


def expand(scalars):
    return scalars[:, :, None, None]


def conjugate(source, first_image, operate, start):
    solution = start
    residual = source
    direction = source
    norm_now = squares(residual)
    applied = first_image
    for iteration in range(ITERS):
        if iteration > 0:
            applied = operate(direction)
        step_size = norm_now / lax.psum(local_sum(direction, applied), "col")
        solution = solution + expand(step_size) * direction
        if iteration + 1 < ITERS:
            residual = residual - expand(step_size) * applied
            norm_next = squares(residual)
            direction = residual + expand(norm_next / norm_now) * direction
            norm_now = norm_next
    return solution


def on_device(
    primary, conductivity, wavenumbers, quadrature, electrodes, far_pole, observed, prior_adjoint
):
    columns = conductivity.shape[0]
    depth_cells = conductivity.shape[1]
    device = lax.axis_index("col")
    device_count = lax.axis_size("col")
    offset = device * columns
    wide_sigma = padded_2(conductivity, (("col", 0),), 2)
    positions = offset - 2 + jnp.arange(columns + 4)
    inside = (positions >= 0) & (positions < columns * device_count)
    contrast_wide = jnp.where(inside[:, None], wide_sigma - 1.0, 0.0)
    mass_scale = (wavenumbers * wavenumbers)[:, None, None, None]
    operator_faces = coefficients(wide_sigma[1:-1])

    def operate(state):
        padded = padded_2(state, (("col", 2),), 1)
        return stencil(padded, operator_faces, mass_scale)

    padded_primary = padded_2(primary, (("col", 2),), 1)
    source = -stencil(padded_primary, coefficients(contrast_wide[1:-1]), mass_scale)
    first_image = operate(source)
    secondary = conjugate(source, first_image, operate, jnp.zeros_like(source))
    total_field = primary + secondary
    surface = total_field[:, :, :, 0]
    weighted = jnp.einsum("k,ksc->sc", quadrature, surface, precision=lax.Precision.HIGHEST)
    pick_table = (electrodes[:, None] - offset == jnp.arange(columns)[None, :]).astype(jnp.float32)
    own_potentials = jnp.einsum("sc,ec->se", weighted, pick_table, precision=lax.Precision.HIGHEST)
    potentials = lax.all_gather(own_potentials, "col", axis=1, tiled=True)
    predicted = potentials - jnp.take_along_axis(potentials, far_pole, axis=1)
    misfit = predicted - observed
    own_count = electrodes.shape[0]
    own_ids = device * own_count + jnp.arange(own_count)
    own_misfit = lax.dynamic_slice_in_dim(misfit, device * own_count, own_count, 1)
    far_hits = (far_pole[:, :, None] == own_ids[None, None, :]).astype(jnp.float32)
    returned = jnp.einsum("sr,sre->se", misfit, far_hits, precision=lax.Precision.HIGHEST)
    charge = own_misfit - returned
    charge_cols = jnp.einsum("se,ec->sc", charge, pick_table, precision=lax.Precision.HIGHEST)
    surface_row = (jnp.arange(depth_cells) == 0).astype(jnp.float32)
    adjoint_source = quadrature[:, None, None, None] * charge_cols[None, :, :, None] * surface_row
    adjoint_residual = adjoint_source - operate(prior_adjoint)
    adjoint = conjugate(adjoint_residual, operate(adjoint_residual), operate, prior_adjoint)
    edge_columns = shifted((adjoint[:, :, :1], total_field[:, :, :1]), "col", -1)
    adjoint_next = jnp.concatenate([adjoint[:, :, 1:], edge_columns[0]], axis=2)
    total_next = jnp.concatenate([total_field[:, :, 1:], edge_columns[1]], axis=2)
    adjoint_down = jnp.concatenate([adjoint[..., 1:], jnp.zeros_like(adjoint[..., :1])], axis=-1)
    total_down = jnp.concatenate(
        [total_field[..., 1:], jnp.zeros_like(total_field[..., :1])], axis=-1
    )
    correlation = (adjoint_next - adjoint) * (total_next - total_field)
    correlation = correlation + (adjoint_down - adjoint) * (total_down - total_field)
    correlation = correlation + mass_scale * adjoint * total_field
    gradient = jnp.sum(correlation, axis=(0, 1))
    return (predicted, gradient)


def solution(mesh):
    placed = (
        P(None, "lines", "col", None),
        P("col", "lines"),
        P(),
        P(),
        P(("lines", "col")),
        P("lines", None),
        P("lines", None),
        P(None, "lines", "col", None),
    )
    return jax.shard_map(
        on_device,
        mesh=mesh,
        in_specs=placed,
        out_specs=(P("lines", None), P("col", "lines")),
        check_vma=False,
    )
```

profile of v0, /device:TPU:0, one launch (start us, length us, event | category | flops | bytes accessed | tf_op | source)
XLA Modules:
  0.0 319.5 jit_solution(12586996976462141782)
XLA Ops:
  1.4 1.3 collective-permute-start.1
  2.7 3.0 collective-permute-start
  6.8 1.3 collective-permute-start.3
  8.1 5.2 %collective-permute-start.2 = (f32[16,2,1,256]{3,2,1,0:T(1,128)S(1)}, f32[16,2,1,256]{3,2,1,0:T(1,128)S(1)}, u32[]{:S(2)}, u32[]{:S(2)}) collective-permute-start(f32[16,2,1,256]{3,2,1,0:T(1,128)S(1)} %get-tuple-element.44), channel_id=1, source_target_pairs={{0,1},{1,2},{2,3},{3,4},{4,5},{5,6},{6,7},{7,8},{8,9},{9,10},{10,1... | collective-permute-start | bytes 98312 | tf_op jit(solution)/shard_map/ppermute | solution.py:14
  14.4 1.3 collective-permute-start.9
  18.9 4.3 %collective-permute-start.8 = (f32[16,2,1,256]{3,2,1,0:T(1,128)S(1)}, f32[16,2,1,256]{3,2,1,0:T(1,128)S(1)}, u32[]{:S(2)}, u32[]{:S(2)}) collective-permute-start(f32[16,2,1,256]{3,2,1,0:T(1,128)S(1)} %get-tuple-element.34), channel_id=1, source_target_pairs={{0,1},{1,2},{2,3},{3,4},{4,5},{5,6},{6,7},{7,8},{8,9},{9,10},{10,1... | collective-permute-start | bytes 98312 | tf_op jit(solution)/shard_map/ppermute | solution.py:14
  23.9 1.3 collective-permute-start.5
  25.2 4.3 %collective-permute-start.4 = (f32[16,2,1,256]{3,2,1,0:T(1,128)S(1)}, f32[16,2,1,256]{3,2,1,0:T(1,128)S(1)}, u32[]{:S(2)}, u32[]{:S(2)}) collective-permute-start(f32[16,2,1,256]{3,2,1,0:T(1,128)S(1)} %get-tuple-element.40), channel_id=1, source_target_pairs={{0,1},{1,2},{2,3},{3,4},{4,5},{5,6},{6,7},{7,8},{8,9},{9,10},{10,1... | collective-permute-start | bytes 98312 | tf_op jit(solution)/shard_map/ppermute | solution.py:14
  30.7 62.1 %all-reduce.19 = (f32[16,2]{1,0:T(8,128)S(1)}, f32[16,2]{1,0:T(8,128)S(1)}) all-reduce(f32[16,2]{1,0:T(8,128)S(1)} %get-tuple-element.13, f32[16,2]{1,0:T(8,128)S(1)} %get-tuple-element.12), channel_id=1, replica_groups=mesh['lines'=2,'col'=16] {'col'}, use_global_device_ids=true, to_apply=%region_1.2 | all-reduce | flops 64 | bytes 512 | tf_op jit(solution)/shard_map/psum | solution.py:58
  93.1 30.0 %psum.58 = f32[16,2]{1,0:T(8,128)S(1)} all-reduce(f32[16,2]{1,0:T(8,128)S(1)} %multiply_reduce_fusion.3), channel_id=1, replica_groups=mesh['lines'=2,'col'=16] {'col'}, use_global_device_ids=true, to_apply=%region_5.6 | all-reduce | flops 32 | bytes 256 | tf_op jit(solution)/shard_map/psum | solution.py:58
  123.3 1.3 collective-permute-start.7
  124.6 3.0 collective-permute-start.6
  128.8 31.3 %psum.59 = f32[16,2]{1,0:T(8,128)S(1)} all-reduce(f32[16,2]{1,0:T(8,128)S(1)} %fusion.55), channel_id=1, replica_groups=mesh['lines'=2,'col'=16] {'col'}, use_global_device_ids=true, to_apply=%region_7.8 | all-reduce | flops 32 | bytes 256 | tf_op jit(solution)/shard_map/psum | solution.py:74
  161.4 17.2 %all-gather = f32[16,2,2]{2,1,0:T(2,128)S(1)} all-gather(f32[1,2,2]{2,1,0:T(2,128)S(1)} %convolution_bitcast_fusion), channel_id=1, replica_groups=mesh['lines'=2,'col'=16] {'col'}, dimensions={0}, use_global_device_ids=true | all-gather | bytes 272 | tf_op jit(solution)/shard_map/all_gather | solution.py:112
  181.6 1.3 collective-permute-start.11
  182.9 3.0 collective-permute-start.10
  186.1 1.3 collective-permute-start.15
  187.9 60.2 %all-reduce.18 = (f32[16,2]{1,0:T(8,128)S(1)}, f32[16,2]{1,0:T(8,128)S(1)}) all-reduce(f32[16,2]{1,0:T(8,128)S(1)} %get-tuple-element.11, f32[16,2]{1,0:T(8,128)S(1)} %get-tuple-element.10), channel_id=1, replica_groups=mesh['lines'=2,'col'=16] {'col'}, use_global_device_ids=true, to_apply=%region_9.10 | all-reduce | flops 64 | bytes 512 | tf_op jit(solution)/shard_map/psum | solution.py:58
  248.3 30.0 %psum.62 = f32[16,2]{1,0:T(8,128)S(1)} all-reduce(f32[16,2]{1,0:T(8,128)S(1)} %multiply_reduce_fusion), channel_id=1, replica_groups=mesh['lines'=2,'col'=16] {'col'}, use_global_device_ids=true, to_apply=%region_13.14 | all-reduce | flops 32 | bytes 256 | tf_op jit(solution)/shard_map/psum | solution.py:58
  278.5 1.3 collective-permute-start.13
  279.8 3.0 collective-permute-start.12
  284.1 31.3 %psum.63 = f32[16,2]{1,0:T(8,128)S(1)} all-reduce(f32[16,2]{1,0:T(8,128)S(1)} %fusion.56), channel_id=1, replica_groups=mesh['lines'=2,'col'=16] {'col'}, use_global_device_ids=true, to_apply=%region_15.16 | all-reduce | flops 32 | bytes 256 | tf_op jit(solution)/shard_map/psum | solution.py:74
  315.6 1.3 collective-permute-start.14
  317.2 1.5 collective-permute-done.14
  (94 shorter events, 17.3 us)
Async XLA Ops:
  0.6 15.1 %copy-start = (f32[16,2,8,256]{3,2,1,0:T(8,128)S(1)}, f32[16,2,8,256]{3,2,1,0:T(8,128)}, u32[]{:S(2)}) copy-start(f32[16,2,8,256]{3,2,1,0:T(8,128)} %param.8) | copy-start | bytes 786436
  1.4 17.5 %collective-permute-start.1 = (f32[2,256]{1,0:T(2,128)S(1)}, f32[2,256]{1,0:T(2,128)S(1)}, u32[]{:S(2)}, u32[]{:S(2)}) collective-permute-start(f32[2,256]{1,0:T(2,128)S(1)} %get-tuple-element.62), channel_id=1, source_target_pairs={{1,0},{2,1},{3,2},{4,3},{5,4},{6,5},{7,6},{8,7},{9,8},{10,9},{11,1... | collective-permute-start | bytes 6152 | tf_op jit(solution)/shard_map/ppermute | solution.py:17
  2.7 20.5 %collective-permute-start = (f32[2,256]{1,0:T(2,128)S(1)}, f32[2,256]{1,0:T(2,128)S(1)}, u32[]{:S(2)}, u32[]{:S(2)}) collective-permute-start(f32[2,256]{1,0:T(2,128)S(1)} %get-tuple-element.61), channel_id=1, source_target_pairs={{0,1},{1,2},{2,3},{3,4},{4,5},{5,6},{6,7},{7,8},{8,9},{9,10},{10,1... | collective-permute-start | bytes 6152 | tf_op jit(solution)/shard_map/ppermute | solution.py:14
  6.8 16.8 %collective-permute-start.3 = (f32[16,2,1,256]{3,2,1,0:T(1,128)S(1)}, f32[16,2,1,256]{3,2,1,0:T(1,128)S(1)}, u32[]{:S(2)}, u32[]{:S(2)}) collective-permute-start(f32[16,2,1,256]{3,2,1,0:T(1,128)S(1)} %get-tuple-element.45), channel_id=1, source_target_pairs={{1,0},{2,1},{3,2},{4,3},{5,4},{6,5},{7,6},{8,7},{9,8},{10,9},{11,1... | collective-permute-start | bytes 98312 | tf_op jit(solution)/shard_map/ppermute | solution.py:17
  8.1 15.5 %collective-permute-start.2 = (f32[16,2,1,256]{3,2,1,0:T(1,128)S(1)}, f32[16,2,1,256]{3,2,1,0:T(1,128)S(1)}, u32[]{:S(2)}, u32[]{:S(2)}) collective-permute-start(f32[16,2,1,256]{3,2,1,0:T(1,128)S(1)} %get-tuple-element.44), channel_id=1, source_target_pairs={{0,1},{1,2},{2,3},{3,4},{4,5},{5,6},{6,7},{7,8},{8,9},{9,10},{10,1... | collective-permute-start | bytes 98312 | tf_op jit(solution)/shard_map/ppermute | solution.py:14
  14.4 166.9 %collective-permute-start.9 = (f32[16,2,1,256]{3,2,1,0:T(1,128)S(1)}, f32[16,2,1,256]{3,2,1,0:T(1,128)S(1)}, u32[]{:S(2)}, u32[]{:S(2)}) collective-permute-start(f32[16,2,1,256]{3,2,1,0:T(1,128)S(1)} %get-tuple-element.35), channel_id=1, source_target_pairs={{1,0},{2,1},{3,2},{4,3},{5,4},{6,5},{7,6},{8,7},{9,8},{10,9},{11,1... | collective-permute-start | bytes 98312 | tf_op jit(solution)/shard_map/ppermute | solution.py:17
  15.7 0.7 copy-start.2
  15.7 1.0 copy-start.1
  16.8 0.7 copy-start.6
  17.5 0.7 copy-start.3
  18.2 0.7 copy-start.7
  18.9 162.4 %collective-permute-start.8 = (f32[16,2,1,256]{3,2,1,0:T(1,128)S(1)}, f32[16,2,1,256]{3,2,1,0:T(1,128)S(1)}, u32[]{:S(2)}, u32[]{:S(2)}) collective-permute-start(f32[16,2,1,256]{3,2,1,0:T(1,128)S(1)} %get-tuple-element.34), channel_id=1, source_target_pairs={{0,1},{1,2},{2,3},{3,4},{4,5},{5,6},{6,7},{7,8},{8,9},{9,10},{10,1... | collective-permute-start | bytes 98312 | tf_op jit(solution)/shard_map/ppermute | solution.py:14
  23.9 5.7 %collective-permute-start.5 = (f32[16,2,1,256]{3,2,1,0:T(1,128)S(1)}, f32[16,2,1,256]{3,2,1,0:T(1,128)S(1)}, u32[]{:S(2)}, u32[]{:S(2)}) collective-permute-start(f32[16,2,1,256]{3,2,1,0:T(1,128)S(1)} %get-tuple-element.41), channel_id=1, source_target_pairs={{1,0},{2,1},{3,2},{4,3},{5,4},{6,5},{7,6},{8,7},{9,8},{10,9},{11,1... | collective-permute-start | bytes 98312 | tf_op jit(solution)/shard_map/ppermute | solution.py:17
  25.2 5.1 %collective-permute-start.4 = (f32[16,2,1,256]{3,2,1,0:T(1,128)S(1)}, f32[16,2,1,256]{3,2,1,0:T(1,128)S(1)}, u32[]{:S(2)}, u32[]{:S(2)}) collective-permute-start(f32[16,2,1,256]{3,2,1,0:T(1,128)S(1)} %get-tuple-element.40), channel_id=1, source_target_pairs={{0,1},{1,2},{2,3},{3,4},{4,5},{5,6},{6,7},{7,8},{8,9},{9,10},{10,1... | collective-permute-start | bytes 98312 | tf_op jit(solution)/shard_map/ppermute | solution.py:14
  123.3 4.5 %collective-permute-start.7 = (f32[16,2,1,256]{3,2,1,0:T(1,128)S(1)}, f32[16,2,1,256]{3,2,1,0:T(1,128)S(1)}, u32[]{:S(2)}, u32[]{:S(2)}) collective-permute-start(f32[16,2,1,256]{3,2,1,0:T(1,128)S(1)} %get-tuple-element.37), channel_id=1, source_target_pairs={{1,0},{2,1},{3,2},{4,3},{5,4},{6,5},{7,6},{8,7},{9,8},{10,9},{11,1... | collective-permute-start | bytes 98312 | tf_op jit(solution)/shard_map/ppermute | solution.py:17
  124.6 3.9 %collective-permute-start.6 = (f32[16,2,1,256]{3,2,1,0:T(1,128)S(1)}, f32[16,2,1,256]{3,2,1,0:T(1,128)S(1)}, u32[]{:S(2)}, u32[]{:S(2)}) collective-permute-start(f32[16,2,1,256]{3,2,1,0:T(1,128)S(1)} %get-tuple-element.36), channel_id=1, source_target_pairs={{0,1},{1,2},{2,3},{3,4},{4,5},{5,6},{6,7},{7,8},{8,9},{9,10},{10,1... | collective-permute-start | bytes 98312 | tf_op jit(solution)/shard_map/ppermute | solution.py:14
  160.3 0.7 copy-start.4
  179.5 0.7 copy-start.5
  181.6 5.8 %collective-permute-start.11 = (f32[16,2,1,256]{3,2,1,0:T(1,128)S(1)}, f32[16,2,1,256]{3,2,1,0:T(1,128)S(1)}, u32[]{:S(2)}, u32[]{:S(2)}) collective-permute-start(f32[16,2,1,256]{3,2,1,0:T(1,128)S(1)} %get-tuple-element.29), channel_id=1, source_target_pairs={{1,0},{2,1},{3,2},{4,3},{5,4},{6,5},{7,6},{8,7},{9,8},{10,9},{11,1... | collective-permute-start | bytes 98312 | tf_op jit(solution)/shard_map/ppermute | solution.py:17
  182.9 4.5 %collective-permute-start.10 = (f32[16,2,1,256]{3,2,1,0:T(1,128)S(1)}, f32[16,2,1,256]{3,2,1,0:T(1,128)S(1)}, u32[]{:S(2)}, u32[]{:S(2)}) collective-permute-start(f32[16,2,1,256]{3,2,1,0:T(1,128)S(1)} %get-tuple-element.28), channel_id=1, source_target_pairs={{0,1},{1,2},{2,3},{3,4},{4,5},{5,6},{6,7},{7,8},{8,9},{9,10},{10,1... | collective-permute-start | bytes 98312 | tf_op jit(solution)/shard_map/ppermute | solution.py:14
  186.1 131.1 %collective-permute-start.15 = (f32[16,2,1,256]{3,2,1,0:T(1,128)S(1)}, f32[16,2,1,256]{3,2,1,0:T(1,128)S(1)}, u32[]{:S(2)}, u32[]{:S(2)}) collective-permute-start(f32[16,2,1,256]{3,2,1,0:T(1,128)S(1)} %slice.268), channel_id=1, source_target_pairs={{1,0},{2,1},{3,2},{4,3},{5,4},{6,5},{7,6},{8,7},{9,8},{10,9},{11,1... | collective-permute-start | bytes 98312 | tf_op jit(solution)/shard_map/ppermute | solution.py:25
  278.5 4.5 %collective-permute-start.13 = (f32[16,2,1,256]{3,2,1,0:T(1,128)S(1)}, f32[16,2,1,256]{3,2,1,0:T(1,128)S(1)}, u32[]{:S(2)}, u32[]{:S(2)}) collective-permute-start(f32[16,2,1,256]{3,2,1,0:T(1,128)S(1)} %get-tuple-element.25), channel_id=1, source_target_pairs={{1,0},{2,1},{3,2},{4,3},{5,4},{6,5},{7,6},{8,7},{9,8},{10,9},{11,1... | collective-permute-start | bytes 98312 | tf_op jit(solution)/shard_map/ppermute | solution.py:17
  279.8 3.9 %collective-permute-start.12 = (f32[16,2,1,256]{3,2,1,0:T(1,128)S(1)}, f32[16,2,1,256]{3,2,1,0:T(1,128)S(1)}, u32[]{:S(2)}, u32[]{:S(2)}) collective-permute-start(f32[16,2,1,256]{3,2,1,0:T(1,128)S(1)} %get-tuple-element.24), channel_id=1, source_target_pairs={{0,1},{1,2},{2,3},{3,4},{4,5},{5,6},{6,7},{7,8},{8,9},{9,10},{10,1... | collective-permute-start | bytes 98312 | tf_op jit(solution)/shard_map/ppermute | solution.py:14
  315.6 3.1 collective-permute-start.14
where the time goes:
time: 320 us; the launch traced here: 319 us
  blocking collectives  262 us (82%)
  starting transfers between devices  37.4 us (12%)
  local copies, waits for them, and re-layouts  9.47 us (3%)
  other arithmetic  4.88 us (2%)
  waiting for transfers between devices  3.56 us (1%)
    psum x4, blocking collectives, squares(): return lax.psum(local_sum(residual, residual), 'col')  182 us
    psum x2, blocking collectives, conjugate(): step_size = norm_now / lax.psum(local_sum(direction, applied), 'col')  62.6 us
    ppermute x7, starting transfers between devices, padded_2(): lax.ppermute(lax.slice_in_dim(block, block.shape[dim] - width, None, axis...  25.8 us
    all_gather x1, blocking collectives, on_device(): potentials = lax.all_gather(own_potentials, 'col', axis=1, tiled=True)  17.2 us
    ppermute x7, starting transfers between devices, padded_2(): lax.ppermute(lax.slice_in_dim(block, 0, width, axis=dim), axis, backward)  9.03 us
  transfers between devices with their start and end apart: 16, of which 4 were waited for; matrix products, arithmetic and copies ran while one was open for 3% of the time, Pallas kernels for 0%

commit v1 on v0

v1 whole, which is shorter than its diff:
```python
import math

import jax
import jax.numpy as jnp
from jax import lax
from jax.sharding import Mesh
from jax.sharding import PartitionSpec as P

ITERS = 2


def halo(block, axis, dim, width):
    count = lax.axis_size(axis)
    edge_shape = list(block.shape)
    edge_shape[dim] = width
    if count == 1:
        zeros = jnp.zeros(edge_shape, block.dtype)
        return jnp.concatenate([zeros, block, zeros], axis=dim)
    forward = [(i, i + 1) for i in range(count - 1)]
    backward = [(target, source) for source, target in forward]
    low = lax.ppermute(
        lax.slice_in_dim(block, block.shape[dim] - width, None, axis=dim), axis, forward
    )
    high = lax.ppermute(lax.slice_in_dim(block, 0, width, axis=dim), axis, backward)
    return jnp.concatenate([low, block, high], axis=dim)


def next_column(field, axis):
    count = lax.axis_size(axis)
    if count == 1:
        edge = jnp.zeros_like(field[:, :, :1])
    else:
        edge = lax.ppermute(field[:, :, :1], axis, [(i + 1, i) for i in range(count - 1)])
    return jnp.concatenate([field[:, :, 1:], edge], axis=2)


def coefficients(sigma_wide):
    center = sigma_wide[1:-1]
    west_face = 0.5 * (center + sigma_wide[:-2])
    east_face = 0.5 * (center + sigma_wide[2:])
    below_sigma = jnp.concatenate([center[:, 1:], jnp.zeros_like(center[:, :1])], axis=1)
    lower_face = 0.5 * (center + below_sigma)
    above_sigma = jnp.concatenate([jnp.zeros_like(center[:, :1]), center[:, :-1]], axis=1)
    upper_face = 0.5 * (center + above_sigma)
    top_row = jnp.arange(center.shape[1]) == 0
    upper_face = jnp.where(top_row[None, :], 0.0, upper_face)
    return (west_face, east_face, lower_face, upper_face, center)


def stencil(field_wide, faces_set, mass_scale):
    west_face, east_face, lower_face, upper_face, center = faces_set
    middle = field_wide[..., 1:-1, :]
    below_cells = jnp.concatenate([middle[..., 1:], jnp.zeros_like(middle[..., :1])], axis=-1)
    above_cells = jnp.concatenate([jnp.zeros_like(middle[..., :1]), middle[..., :-1]], axis=-1)
    result = west_face * (middle - field_wide[..., :-2, :]) + east_face * (
        middle - field_wide[..., 2:, :]
    )
    result = result + lower_face * (middle - below_cells) + upper_face * (middle - above_cells)
    return result + mass_scale * center * middle


def on_device(
    primary, conductivity, wavenumbers, quadrature, electrodes, far_pole, observed, prior_adjoint
):
    groups = lax.axis_size("kq")
    spread = lax.axis_size("cs")
    waves, sources, own_columns, depth = primary.shape
    per_group = waves // groups
    group = lax.axis_index("kq")
    block = lax.axis_index("cs")
    fields = per_group * sources

    def by_group(array):
        return array.reshape(groups, fields, own_columns, depth)

    sigma_copies = jnp.broadcast_to(conductivity[None, None], (groups, 1, own_columns, depth))
    send = jnp.concatenate([by_group(primary), by_group(prior_adjoint), sigma_copies], axis=1)
    if groups > 1:
        send = lax.all_to_all(send, "kq", 0, 2, tiled=True)
    received = send[0]
    width = groups * own_columns
    primary = received[:fields].reshape(per_group, sources, width, depth)
    prior_adjoint = received[fields : 2 * fields].reshape(per_group, sources, width, depth)
    sigma = received[2 * fields]

    columns = width * spread
    offset = block * width
    wide_sigma = halo(sigma, "cs", 0, 2)
    positions = offset - 2 + jnp.arange(width + 4)
    inside = (positions >= 0) & (positions < columns)
    contrast_wide = jnp.where(inside[:, None], wide_sigma - 1.0, 0.0)
    own_waves = lax.dynamic_slice_in_dim(wavenumbers, group * per_group, per_group)
    weights = lax.dynamic_slice_in_dim(quadrature, group * per_group, per_group)
    mass_scale = (own_waves * own_waves)[:, None, None, None]
    operator_faces = coefficients(wide_sigma[1:-1])

    def operate(state):
        return stencil(halo(state, "cs", 2, 1), operator_faces, mass_scale)

    def dots(left, right):
        total = jnp.sum(left * right, axis=(2, 3))
        if spread > 1:
            total = lax.psum(total, "cs")
        return total[:, :, None, None]

    def conjugate(source, start):
        if start is None:
            solution = jnp.zeros_like(source)
            residual = source
        else:
            solution = start
            residual = source - operate(start)
        direction = residual
        norm_now = dots(residual, residual)
        for iteration in range(ITERS):
            applied = operate(direction)
            step_size = norm_now / dots(direction, applied)
            solution = solution + step_size * direction
            if iteration + 1 < ITERS:
                residual = residual - step_size * applied
                norm_next = dots(residual, residual)
                direction = residual + (norm_next / norm_now) * direction
                norm_now = norm_next
        return solution

    source = -stencil(halo(primary, "cs", 2, 1), coefficients(contrast_wide[1:-1]), mass_scale)
    total_field = primary + conjugate(source, None)

    surface = total_field[:, :, :, 0]
    weighted = jnp.sum(weights[:, None, None] * surface, axis=0)
    packet = jnp.concatenate([weighted.reshape(-1), electrodes.astype(jnp.float32)])
    gathered = lax.all_gather(packet, ("cs", "kq"))
    partial = gathered[:, : sources * width].reshape(spread, groups, sources, width)
    line_surface = jnp.sum(partial, axis=1).transpose(1, 0, 2).reshape(sources, columns)
    all_electrodes = gathered[:, sources * width :].reshape(-1).astype(jnp.int32)
    count = all_electrodes.shape[0]

    picks = (all_electrodes[:, None] == jnp.arange(columns)[None, :]).astype(jnp.float32)
    potentials = jnp.sum(line_surface[:, None, :] * picks[None], axis=2)
    pole_hits = (far_pole[:, :, None] == jnp.arange(count)[None, None, :]).astype(jnp.float32)
    far_potentials = jnp.sum(potentials[:, None, :] * pole_hits, axis=2)
    predicted = potentials - far_potentials
    misfit = predicted - observed
    returned = jnp.sum(misfit[:, :, None] * pole_hits, axis=1)
    charge = misfit - returned
    own_picks = (
        all_electrodes[:, None] == offset + jnp.arange(width)[None, :]
    ).astype(jnp.float32)
    charge_cols = jnp.sum(charge[:, :, None] * own_picks[None], axis=1)
    surface_row = (jnp.arange(depth) == 0).astype(jnp.float32)
    adjoint_source = weights[:, None, None, None] * charge_cols[None, :, :, None] * surface_row
    adjoint = conjugate(adjoint_source, prior_adjoint)

    adjoint_next = next_column(adjoint, "cs")
    total_next = next_column(total_field, "cs")
    adjoint_down = jnp.concatenate([adjoint[..., 1:], jnp.zeros_like(adjoint[..., :1])], axis=-1)
    total_down = jnp.concatenate(
        [total_field[..., 1:], jnp.zeros_like(total_field[..., :1])], axis=-1
    )
    correlation = (adjoint_next - adjoint) * (total_next - total_field)
    correlation = correlation + (adjoint_down - adjoint) * (total_down - total_field)
    correlation = correlation + mass_scale * adjoint * total_field
    gradient = jnp.sum(correlation, axis=(0, 1))
    if groups > 1:
        gradient = lax.psum_scatter(gradient, "kq", scatter_dimension=0, tiled=True)
    return (predicted, gradient)


def solution(mesh):
    lines = mesh.shape["lines"]
    col = mesh.shape["col"]

    def run(*arrays):
        groups = math.gcd(col, arrays[0].shape[0])
        split = Mesh(mesh.devices.reshape(lines, col // groups, groups), ("lines", "cs", "kq"))
        cells = ("cs", "kq")
        placed = (
            P(None, "lines", cells, None),
            P(cells, "lines"),
            P(),
            P(),
            P(("lines",) + cells),
            P("lines", None),
            P("lines", None),
            P(None, "lines", cells, None),
        )
        return jax.shard_map(
            on_device,
            mesh=split,
            in_specs=placed,
            out_specs=(P("lines", None), P(cells, "lines")),
            check_vma=False,
        )(*arrays)

    return run
```

time: 320 us -> 164 us (0.51)
  blocking collectives: 262 us -> 60.8 us
  waiting for transfers between devices: 3.56 us -> 63.8 us
  starting transfers between devices: 37.4 us -> 7.45 us
  between operations: 1.21 us -> 16.3 us
  other arithmetic: 4.88 us -> 8.09 us
    psum x6 -> x0, blocking collectives: 245 us -> none  [the longest x4 182 us: squares(): return lax.psum(local_sum(residual, residual), 'col')]
    unnamed x0 -> x1, blocking collectives: none -> 60.8 us
    reduce_scatter x0 -> x1, waiting for transfers between devices: none -> 53 us  [on_device(): gradient = lax.psum_scatter(gradient, 'kq', scatter_dimension=0, tiled=True)]
    ppermute x16 -> x0, starting transfers between devices: 37.4 us -> none  [the longest x7 25.8 us: padded_2(): lax.ppermute(lax.slice_in_dim(block, block.shape[dim] - width, None, axis...]
    all_gather x1 -> x0, blocking collectives: 17.2 us -> none  [on_device(): potentials = lax.all_gather(own_potentials, 'col', axis=1, tiled=True)]
    all_to_all x0 -> x1, waiting for transfers between devices: none -> 10.8 us  [on_device(): send = lax.all_to_all(send, 'kq', 0, 2, tiled=True)]
    all_to_all x0 -> x1, starting transfers between devices: none -> 7.41 us  [on_device(): send = lax.all_to_all(send, 'kq', 0, 2, tiled=True)]
    ppermute x16 -> x0, waiting for transfers between devices: 3.56 us -> none  [the longest x7 2.08 us: padded_2(): lax.ppermute(lax.slice_in_dim(block, block.shape[dim] - width, None, axis...]
  transfers between devices with their start and end apart: 16 -> 2, of which waited for: 4 -> 2; matrix products, arithmetic and copies ran while one was open for 3% -> 1% of each run, Pallas kernels for 0% -> 0%
where the time goes in v1:
time: 164 us; the launch traced here: 163 us
  waiting for transfers between devices  63.8 us (39%)
  blocking collectives  60.8 us (37%)
  between operations  16.3 us (10%)
  other arithmetic  8.09 us (5%)
  starting transfers between devices  7.45 us (5%)
  local copies, waits for them, and re-layouts  7.03 us (4%)
    unnamed x1, blocking collectives  60.8 us
    reduce_scatter x1, waiting for transfers between devices, on_device(): gradient = lax.psum_scatter(gradient, 'kq', scatter_dimension=0, tiled=True)  53 us
    all_to_all x1, waiting for transfers between devices, on_device(): send = lax.all_to_all(send, 'kq', 0, 2, tiled=True)  10.8 us
    all_to_all x1, starting transfers between devices, on_device(): send = lax.all_to_all(send, 'kq', 0, 2, tiled=True)  7.41 us
    unnamed x14, local copies, waits for them, and re-layouts  3.66 us
  transfers between devices with their start and end apart: 2, of which 2 were waited for; matrix products, arithmetic and copies ran while one was open for 1% of the time, Pallas kernels for 0%

profile of v1, /device:TPU:0, one launch (start us, length us, event | category | flops | bytes accessed | tf_op | source)
XLA Modules:
  0.0 163.5 jit_solution(5212997132904193159)
XLA Ops:
  7.2 0.7 broadcast_in_dim.34
  7.9 1.9 %pad_maximum_fusion = f32[16,5,8,256]{3,2,1,0:T(8,128)} fusion(f32[16,1,8,256]{3,2,1,0:T(8,128)S(1)} %broadcast_in_dim.34, f32[16,2,8,256]{3,2,1,0:T(8,128)} %param.15, f32[16,2,8,256]{3,2,1,0:T(8,128)} %param.8), kind=kLoop, calls=%fused_computation | loop fusion | flops 327680 | bytes 1310720 | tf_op jit(solution)/shard_map/concatenate | solution.py:77
  9.8 7.4 %all-to-all-start = ((f32[16,5,8,256]{3,2,1,0:T(8,128)}), f32[16,5,8,256]{3,2,1,0:T(8,128)S(1)}, u32[]{:S(2)}, u32[]{:S(2)}) async-start(f32[16,5,8,256]{3,2,1,0:T(8,128)} %pad_maximum_fusion), calls=%async_computation | async-start | bytes 1310720 | tf_op jit(solution)/shard_map/all_to_all | solution.py:79
  17.3 0.6 copy-done.2
  17.9 0.6 dynamic_slice.7
  19.8 0.6 dynamic_slice.6
  20.4 0.7 copy-done.4
  21.1 0.7 copy-done.5
  21.8 0.6 dynamic-slice
  23.0 10.8 %all-to-all-done = f32[16,5,8,256]{3,2,1,0:T(8,128)S(1)} async-done(((f32[16,5,8,256]{3,2,1,0:T(8,128)}), f32[16,5,8,256]{3,2,1,0:T(8,128)S(1)}, u32[]{:S(2)}, u32[]{:S(2)}) %all-to-all-start) | async-done | bytes 655392 | tf_op jit(solution)/shard_map/all_to_all | solution.py:79
  35.0 0.3 multiply_reduce_fusion.4
  35.3 0.2 multiply_reduce_fusion.3
  35.8 0.3 fusion.52
  36.2 0.7 fusion.58
  37.1 60.8 %all-reduce.34 = f32[4128]{0:T(1024)S(1)} all-reduce(f32[4128]{0:T(1024)S(1)} %maximum_dynamic-update-slice_fusion), channel_id=2, replica_groups=mesh['lines'=2,'col'=16] {'col'}, use_global_device_ids=true, to_apply=%add.34 | all-reduce | flops 4128 | bytes 33024
  98.3 0.6 copy-done
  99.0 0.5 copy-done.1
  99.5 0.6 fusion.64
  100.3 0.6 broadcast_multiply_fusion.1
  101.3 0.3 multiply_reduce_fusion.1
  101.6 0.2 multiply_reduce_fusion
  102.1 0.3 fusion.51
  102.8 0.8 add_reduce_fusion
  103.6 53.0 %reduce-scatter.2.cloned.1.call-done = f32[8,256]{1,0:T(8,128)} async-done(((f32[128,256]{1,0:T(8,128)}), f32[8,256]{1,0:T(8,128)}) %reduce-scatter.2.cloned.1.call-update) | async-done | bytes 8208 | tf_op jit(solution)/shard_map/reduce_scatter | solution.py:165
  (55 shorter events, 3.4 us)
Async XLA Ops:
  9.8 24.0 %all-to-all-start = ((f32[16,5,8,256]{3,2,1,0:T(8,128)}), f32[16,5,8,256]{3,2,1,0:T(8,128)S(1)}, u32[]{:S(2)}, u32[]{:S(2)}) async-start(f32[16,5,8,256]{3,2,1,0:T(8,128)} %pad_maximum_fusion), calls=%async_computation | async-start | bytes 1310720 | tf_op jit(solution)/shard_map/all_to_all | solution.py:79
  17.2 139.4 %reduce-scatter.2.cloned.1.call-start = ((), (), s32[]{:S(2)}) async-start(), calls=%async_computation.2 | async-start | bytes 139264 | tf_op jit(solution)/shard_map/reduce_scatter | solution.py:165
  17.3 0.7 copy-start.2
  18.5 1.3 copy-start.3
  20.4 0.7 copy-start.4
  21.1 0.7 copy-start.5
  98.2 0.7 copy-start
  98.8 0.7 copy-start.1
Sparse Core Ops, SparseCore 0:
  103.7 52.8 reduce-scatter.1

commit v2 on v1

--- a/solution.py
+++ b/solution.py
@@ -129,7 +129,12 @@
     surface = total_field[:, :, :, 0]
     weighted = jnp.sum(weights[:, None, None] * surface, axis=0)
     packet = jnp.concatenate([weighted.reshape(-1), electrodes.astype(jnp.float32)])
-    gathered = lax.all_gather(packet, ("cs", "kq"))
+    gathered = jnp.broadcast_to(packet[None], (groups,) + packet.shape)
+    if groups > 1:
+        gathered = lax.all_to_all(gathered, "kq", 0, 0, tiled=True)
+    if spread > 1:
+        gathered = lax.all_gather(gathered, "cs")
+    gathered = gathered.reshape(spread * groups, -1)
     partial = gathered[:, : sources * width].reshape(spread, groups, sources, width)
     line_surface = jnp.sum(partial, axis=1).transpose(1, 0, 2).reshape(sources, columns)
     all_electrodes = gathered[:, sources * width :].reshape(-1).astype(jnp.int32)
@@ -162,7 +167,8 @@
     correlation = correlation + mass_scale * adjoint * total_field
     gradient = jnp.sum(correlation, axis=(0, 1))
     if groups > 1:
-        gradient = lax.psum_scatter(gradient, "kq", scatter_dimension=0, tiled=True)
+        gradient = gradient.reshape(groups, own_columns, depth)
+        gradient = jnp.sum(lax.all_to_all(gradient, "kq", 0, 0, tiled=True), axis=0)
     return (predicted, gradient)
 
 

time: 164 us -> 58.6 us (0.36)
  blocking collectives: 60.8 us -> 10.5 us
  waiting for transfers between devices: 63.8 us -> 19.7 us
  between operations: 16.3 us -> 2.23 us
  starting transfers between devices: 7.45 us -> 12.1 us
    unnamed x1 -> x0, blocking collectives: 60.8 us -> none
    reduce_scatter x1 -> x0, waiting for transfers between devices: 53 us -> none  [on_device(): gradient = lax.psum_scatter(gradient, 'kq', scatter_dimension=0, tiled=True)]
    all_to_all x0 -> x1, blocking collectives: none -> 10.5 us  [on_device(): gradient = jnp.sum(lax.all_to_all(gradient, 'kq', 0, 0, tiled=True), axis=0)]
    all_to_all x0 -> x1, waiting for transfers between devices: none -> 6.4 us  [on_device(): gathered = lax.all_to_all(gathered, 'kq', 0, 0, tiled=True)]
    all_to_all x0 -> x1, starting transfers between devices: none -> 4.67 us  [on_device(): gathered = lax.all_to_all(gathered, 'kq', 0, 0, tiled=True)]
    all_to_all x1, waiting for transfers between devices: 10.8 us -> 13.3 us  [on_device(): send = lax.all_to_all(send, 'kq', 0, 2, tiled=True)]
    unnamed x14 -> x11, local copies, waits for them, and re-layouts: 3.66 us -> 1.83 us
  transfers between devices with their start and end apart: 2 -> 2, of which waited for: 2 -> 2; matrix products, arithmetic and copies ran while one was open for 1% -> 2% of each run, Pallas kernels for 0% -> 0%
where the time goes in v2:
time: 58.6 us; the launch traced here: 58.2 us
  waiting for transfers between devices  19.7 us (34%)
  starting transfers between devices  12.1 us (21%)
  blocking collectives  10.5 us (18%)
  other arithmetic  7.94 us (14%)
  local copies, waits for them, and re-layouts  5.71 us (10%)
  between operations  2.23 us (4%)
    all_to_all x1, waiting for transfers between devices, on_device(): send = lax.all_to_all(send, 'kq', 0, 2, tiled=True)  13.3 us
    all_to_all x1, blocking collectives, on_device(): gradient = jnp.sum(lax.all_to_all(gradient, 'kq', 0, 0, tiled=True), axis=0)  10.5 us
    all_to_all x1, starting transfers between devices, on_device(): send = lax.all_to_all(send, 'kq', 0, 2, tiled=True)  7.41 us
    all_to_all x1, waiting for transfers between devices, on_device(): gathered = lax.all_to_all(gathered, 'kq', 0, 0, tiled=True)  6.4 us
    all_to_all x1, starting transfers between devices, on_device(): gathered = lax.all_to_all(gathered, 'kq', 0, 0, tiled=True)  4.67 us
    concatenate x1, other arithmetic, on_device(): jnp.concatenate([by_group(primary), by_group(prior_adjoint), sigma_copies...  1.93 us
    unnamed x11, local copies, waits for them, and re-layouts  1.83 us
    reduce_sum x6, other arithmetic, dots(): total = jnp.sum(left * right, axis=(2, 3))  1.63 us
  transfers between devices with their start and end apart: 2, of which 2 were waited for; matrix products, arithmetic and copies ran while one was open for 2% of the time, Pallas kernels for 0%

profile of v2, /device:TPU:0, one launch (start us, length us, event | category | flops | bytes accessed | tf_op | source)
XLA Modules:
  0.0 58.2 jit_solution(2509714716856412962)
XLA Ops:
  0.6 0.7 %broadcast_in_dim.36 = f32[16,1,8,256]{3,2,1,0:T(8,128)S(1)} broadcast(f32[8,256]{1,0:T(8,128)} %param.9), dimensions={2,3} | broadcast | bytes 139264 | tf_op jit(solution)/shard_map/broadcast_in_dim | solution.py:76
  1.3 1.9 %pad_maximum_fusion = f32[16,5,8,256]{3,2,1,0:T(8,128)} fusion(f32[16,1,8,256]{3,2,1,0:T(8,128)S(1)} %broadcast_in_dim.36, f32[16,2,8,256]{3,2,1,0:T(8,128)} %param.15, f32[16,2,8,256]{3,2,1,0:T(8,128)} %param.8), kind=kLoop, calls=%fused_computation | loop fusion | flops 327680 | bytes 1310720 | tf_op jit(solution)/shard_map/concatenate | solution.py:77
  3.3 7.4 %all-to-all-start = ((f32[16,5,8,256]{3,2,1,0:T(8,128)}), f32[16,5,8,256]{3,2,1,0:T(8,128)S(1)}, u32[]{:S(2)}, u32[]{:S(2)}) async-start(f32[16,5,8,256]{3,2,1,0:T(8,128)} %pad_maximum_fusion), calls=%async_computation | async-start | bytes 1310720 | tf_op jit(solution)/shard_map/all_to_all | solution.py:79
  10.7 0.6 %copy-done.2 = f32[16]{0:T(128)S(1)} copy-done((f32[16]{0:T(128)S(1)}, f32[16]{0:T(128)}, u32[]{:S(2)}) %copy-start.2) | copy-done | bytes 88
  11.4 0.6 %dynamic_slice.7 = f32[1]{0:T(128)} dynamic-slice(f32[16]{0:T(128)S(1)} %copy-done.2, s32[]{:T(128)S(6)} %select_n.15), dynamic_slice_sizes={1} | dynamic-slice | bytes 12 | tf_op jit(solution)/shard_map/dynamic_slice | solution.py:92
  13.3 0.6 %dynamic_slice.6 = f32[1]{0:T(128)} dynamic-slice(f32[16]{0:T(128)S(1)} %copy-done.3, s32[]{:T(128)S(6)} %select_n.15), dynamic_slice_sizes={1} | dynamic-slice | bytes 12 | tf_op jit(solution)/shard_map/dynamic_slice | solution.py:93
  13.9 13.3 %all-to-all-done = f32[16,5,8,256]{3,2,1,0:T(8,128)S(1)} async-done(((f32[16,5,8,256]{3,2,1,0:T(8,128)}), f32[16,5,8,256]{3,2,1,0:T(8,128)S(1)}, u32[]{:S(2)}, u32[]{:S(2)}) %all-to-all-start) | async-done | bytes 655392 | tf_op jit(solution)/shard_map/all_to_all | solution.py:79
  27.7 0.2 fusion.70
  28.4 0.3 multiply_reduce_fusion.4
  28.8 0.2 multiply_reduce_fusion.3
  29.3 0.3 fusion.52
  29.7 0.7 %fusion.58 = f32[2,128]{1,0:T(2,128)S(1)} fusion(f32[1,2,128,256]{3,2,1,0:T(8,128)S(1)} %add_add_fusion, f32[]{:T(128)} %bitcast), kind=kLoop, calls=%fused_computation.91 | loop fusion | flops 256 | bytes 2052 | tf_op jit(solution)/shard_map/mul | solution.py:130
  30.4 0.6 %broadcast_in_dim.42 = f32[16,1,258]{2,1,0:T(1,128)} broadcast(f32[258]{0:T(512)S(1)} %pad_maximum_fusion.1), dimensions={2} | broadcast | bytes 17544 | tf_op jit(solution)/shard_map/broadcast_in_dim | solution.py:132
  31.0 4.7 %all-to-all-start.1 = ((f32[16,1,258]{2,1,0:T(1,128)}), f32[16,1,258]{2,1,0:T(1,128)S(1)}, u32[]{:S(2)}, u32[]{:S(2)}) async-start(f32[16,1,258]{2,1,0:T(1,128)} %broadcast_in_dim.42), calls=%async_computation.1 | async-start | bytes 49152 | tf_op jit(solution)/shard_map/all_to_all | solution.py:134
  35.9 6.4 %all-to-all-done.1 = f32[16,1,258]{2,1,0:T(1,128)S(1)} async-done(((f32[16,1,258]{2,1,0:T(1,128)}), f32[16,1,258]{2,1,0:T(1,128)S(1)}, u32[]{:S(2)}, u32[]{:S(2)}) %all-to-all-start.1) | async-done | bytes 16544 | tf_op jit(solution)/shard_map/all_to_all | solution.py:134
  42.6 0.6 %copy-done = s32[2,32]{1,0:T(2,128)S(1)} copy-done((s32[2,32]{1,0:T(2,128)S(1)}, s32[2,32]{1,0:T(2,128)}, u32[]{:S(2)}) %copy-start) | copy-done | bytes 280
  43.3 0.5 copy-done.1
  43.8 0.6 fusion.64
  44.6 0.6 %broadcast_multiply_fusion.1 = f32[2,128]{1,0:T(2,128)S(1)} fusion(f32[2,128]{1,0:T(2,128)S(1)} %multiply_reduce_fusion.6, f32[]{:T(128)} %bitcast), kind=kLoop, calls=%fused_computation.116 | loop fusion | flops 256 | bytes 2052 | tf_op jit(solution)/shard_map/mul | solution.py:156
  45.6 0.3 multiply_reduce_fusion.1
  45.9 0.2 multiply_reduce_fusion
  46.4 0.3 fusion.51
  47.1 10.5 %all_to_all.29 = f32[16,8,256]{2,1,0:T(8,128)S(1)} all-to-all(f32[16,8,256]{2,1,0:T(8,128)S(1)} %bitcast.34), channel_id=1, replica_groups=mesh['lines'=2,'col'=16] {'col'}, dimensions={0} | all-to-all | bytes 262144 | tf_op jit(solution)/shard_map/all_to_all | solution.py:171
  57.6 0.6 %reduce_sum.153 = f32[8,256]{1,0:T(8,128)} reduce(f32[16,8,256]{2,1,0:T(8,128)S(1)} %all_to_all.29, f32[]{:T(128)} %constant.15.clone.1), dimensions={0}, to_apply=%region_14.15 | reduce | flops 30720 | bytes 139268 | tf_op jit(solution)/shard_map/reduce_sum | solution.py:171
  (52 shorter events, 3.1 us)
Async XLA Ops:
  3.3 24.0 %all-to-all-start = ((f32[16,5,8,256]{3,2,1,0:T(8,128)}), f32[16,5,8,256]{3,2,1,0:T(8,128)S(1)}, u32[]{:S(2)}, u32[]{:S(2)}) async-start(f32[16,5,8,256]{3,2,1,0:T(8,128)} %pad_maximum_fusion), calls=%async_computation | async-start | bytes 1310720 | tf_op jit(solution)/shard_map/all_to_all | solution.py:79
  10.7 0.7 %copy-start.2 = (f32[16]{0:T(128)S(1)}, f32[16]{0:T(128)}, u32[]{:S(2)}) copy-start(f32[16]{0:T(128)} %param.10) | copy-start | bytes 196
  11.9 1.3 %copy-start.3 = (f32[16]{0:T(128)S(1)}, f32[16]{0:T(128)}, u32[]{:S(2)}) copy-start(f32[16]{0:T(128)} %param.11) | copy-start | bytes 196
  13.3 0.7 %copy-start.4 = (s32[2]{0:T(128)S(1)}, s32[2]{0:T(128)}, u32[]{:S(2)}) copy-start(s32[2]{0:T(128)} %param.12) | copy-start | bytes 28
  31.0 11.2 %all-to-all-start.1 = ((f32[16,1,258]{2,1,0:T(1,128)}), f32[16,1,258]{2,1,0:T(1,128)S(1)}, u32[]{:S(2)}, u32[]{:S(2)}) async-start(f32[16,1,258]{2,1,0:T(1,128)} %broadcast_in_dim.42), calls=%async_computation.1 | async-start | bytes 49152 | tf_op jit(solution)/shard_map/all_to_all | solution.py:134
  42.5 0.7 %copy-start = (s32[2,32]{1,0:T(2,128)S(1)}, s32[2,32]{1,0:T(2,128)}, u32[]{:S(2)}) copy-start(s32[2,32]{1,0:T(2,128)} %param.13) | copy-start | bytes 772
  43.2 0.7 %copy-start.1 = (f32[2,32]{1,0:T(2,128)S(1)}, f32[2,32]{1,0:T(2,128)}, u32[]{:S(2)}) copy-start(f32[2,32]{1,0:T(2,128)} %param.14) | copy-start | bytes 772

commit v3 on v2

--- a/solution.py
+++ b/solution.py
@@ -68,20 +68,14 @@
     per_group = waves // groups
     group = lax.axis_index("kq")
     block = lax.axis_index("cs")
-    fields = per_group * sources
 
-    def by_group(array):
-        return array.reshape(groups, fields, own_columns, depth)
-
-    sigma_copies = jnp.broadcast_to(conductivity[None, None], (groups, 1, own_columns, depth))
-    send = jnp.concatenate([by_group(primary), by_group(prior_adjoint), sigma_copies], axis=1)
+    width = groups * own_columns
+    sigma = jnp.broadcast_to(conductivity[None], (groups, own_columns, depth))
     if groups > 1:
-        send = lax.all_to_all(send, "kq", 0, 2, tiled=True)
-    received = send[0]
-    width = groups * own_columns
-    primary = received[:fields].reshape(per_group, sources, width, depth)
-    prior_adjoint = received[fields : 2 * fields].reshape(per_group, sources, width, depth)
-    sigma = received[2 * fields]
+        primary = lax.all_to_all(primary, "kq", 0, 2, tiled=True)
+        sigma = lax.all_to_all(sigma, "kq", 0, 1, tiled=True)
+        prior_adjoint = lax.all_to_all(prior_adjoint, "kq", 0, 2, tiled=True)
+    sigma = sigma[0]
 
     columns = width * spread
     offset = block * width

time: 58.6 us -> 71.5 us (1.22)
  waiting for transfers between devices: 19.7 us -> 27.9 us
  starting transfers between devices: 12.1 us -> 18 us
  other arithmetic: 7.94 us -> 5.92 us
    all_to_all x1 -> x3, waiting for transfers between devices: 13.3 us -> 21.7 us  [the longest x1 9.44 us: on_device(): primary = lax.all_to_all(primary, 'kq', 0, 2, tiled=True)]
    all_to_all x1 -> x3, starting transfers between devices: 7.41 us -> 14.5 us  [the longest x1 7.41 us: on_device(): sigma = lax.all_to_all(sigma, 'kq', 0, 1, tiled=True)]
    concatenate x1 -> x0, other arithmetic: 1.93 us -> none  [on_device(): jnp.concatenate([by_group(primary), by_group(prior_adjoint), sigma_copies...]
    all_to_all x1, starting transfers between devices: 4.67 us -> 3.49 us  [on_device(): gathered = lax.all_to_all(gathered, 'kq', 0, 0, tiled=True)]
  transfers between devices with their start and end apart: 2 -> 4, of which waited for: 2 -> 4; matrix products, arithmetic and copies ran while one was open for 2% -> 6% of each run, Pallas kernels for 0% -> 0%
where the time goes in v3:
time: 71.5 us; the launch traced here: 70.8 us
  waiting for transfers between devices  27.9 us (39%)
  starting transfers between devices  18 us (25%)
  blocking collectives  10.5 us (15%)
  local copies, waits for them, and re-layouts  6.33 us (9%)
  other arithmetic  5.92 us (8%)
  between operations  2.24 us (3%)
    all_to_all x1, blocking collectives, on_device(): gradient = jnp.sum(lax.all_to_all(gradient, 'kq', 0, 0, tiled=True), axis=0)  10.5 us
    all_to_all x1, waiting for transfers between devices, on_device(): primary = lax.all_to_all(primary, 'kq', 0, 2, tiled=True)  9.44 us
    all_to_all x1, waiting for transfers between devices, on_device(): prior_adjoint = lax.all_to_all(prior_adjoint, 'kq', 0, 2, tiled=True)  7.56 us
    all_to_all x1, starting transfers between devices, on_device(): sigma = lax.all_to_all(sigma, 'kq', 0, 1, tiled=True)  7.41 us
    all_to_all x1, waiting for transfers between devices, on_device(): gathered = lax.all_to_all(gathered, 'kq', 0, 0, tiled=True)  6.21 us
    all_to_all x1, waiting for transfers between devices, on_device(): sigma = lax.all_to_all(sigma, 'kq', 0, 1, tiled=True)  4.65 us
    all_to_all x1, starting transfers between devices, on_device(): primary = lax.all_to_all(primary, 'kq', 0, 2, tiled=True)  3.53 us
    all_to_all x1, starting transfers between devices, on_device(): prior_adjoint = lax.all_to_all(prior_adjoint, 'kq', 0, 2, tiled=True)  3.53 us
  transfers between devices with their start and end apart: 4, of which 4 were waited for; matrix products, arithmetic and copies ran while one was open for 6% of the time, Pallas kernels for 0%

profile of v3, /device:TPU:0, one launch (start us, length us, event | category | flops | bytes accessed | tf_op | source)
XLA Modules:
  0.0 70.8 jit_solution(17949879009757526271)
XLA Ops:
  0.6 1.3 %broadcast_in_dim.38 = f32[16,8,256]{2,1,0:T(8,128)} broadcast(f32[8,256]{1,0:T(8,128)} %param.9), dimensions={1,2} | broadcast | bytes 139264 | tf_op jit(solution)/shard_map/broadcast_in_dim | solution.py:73
  2.0 7.4 %all-to-all-start.1 = ((f32[16,8,256]{2,1,0:T(8,128)}), f32[16,8,256]{2,1,0:T(8,128)S(1)}, u32[]{:S(2)}, u32[]{:S(2)}) async-start(f32[16,8,256]{2,1,0:T(8,128)} %broadcast_in_dim.38), calls=%async_computation.1 | async-start | bytes 262144 | tf_op jit(solution)/shard_map/all_to_all | solution.py:76
  9.4 0.6 copy-done.2
  10.1 0.6 dynamic_slice.7
  12.0 0.6 dynamic_slice.6
  12.6 4.6 %all-to-all-done.1 = f32[16,8,256]{2,1,0:T(8,128)S(1)} async-done(((f32[16,8,256]{2,1,0:T(8,128)}), f32[16,8,256]{2,1,0:T(8,128)S(1)}, u32[]{:S(2)}, u32[]{:S(2)}) %all-to-all-start.1) | async-done | bytes 131104 | tf_op jit(solution)/shard_map/all_to_all | solution.py:76
  17.3 3.5 %all-to-all-start = ((f32[16,2,8,256]{3,2,1,0:T(8,128)}), f32[16,2,8,256]{3,2,1,0:T(8,128)S(1)}, u32[]{:S(2)}, u32[]{:S(2)}) async-start(f32[16,2,8,256]{3,2,1,0:T(8,128)} %param.8), calls=%async_computation | async-start | bytes 524288 | tf_op jit(solution)/shard_map/all_to_all | solution.py:75
  21.4 9.4 %all-to-all-done = f32[16,2,8,256]{3,2,1,0:T(8,128)S(1)} async-done(((f32[16,2,8,256]{3,2,1,0:T(8,128)}), f32[16,2,8,256]{3,2,1,0:T(8,128)S(1)}, u32[]{:S(2)}, u32[]{:S(2)}) %all-to-all-start) | async-done | bytes 262176 | tf_op jit(solution)/shard_map/all_to_all | solution.py:75
  30.8 3.5 %all-to-all-start.3 = ((f32[16,2,8,256]{3,2,1,0:T(8,128)}), f32[16,2,8,256]{3,2,1,0:T(8,128)S(1)}, u32[]{:S(2)}, u32[]{:S(2)}) async-start(f32[16,2,8,256]{3,2,1,0:T(8,128)} %param.15), calls=%async_computation.3 | async-start | bytes 524288 | tf_op jit(solution)/shard_map/all_to_all | solution.py:77
  34.9 0.3 multiply_reduce_fusion.4
  35.7 0.3 fusion.52
  36.1 0.7 fusion.58
  36.8 7.6 %all-to-all-done.3 = f32[16,2,8,256]{3,2,1,0:T(8,128)S(1)} async-done(((f32[16,2,8,256]{3,2,1,0:T(8,128)}), f32[16,2,8,256]{3,2,1,0:T(8,128)S(1)}, u32[]{:S(2)}, u32[]{:S(2)}) %all-to-all-start.3) | async-done | bytes 262176 | tf_op jit(solution)/shard_map/all_to_all | solution.py:77
  44.3 0.6 broadcast_in_dim.42
  44.9 3.5 %all-to-all-start.2 = ((f32[16,1,258]{2,1,0:T(1,128)}), f32[16,1,258]{2,1,0:T(1,128)S(1)}, u32[]{:S(2)}, u32[]{:S(2)}) async-start(f32[16,1,258]{2,1,0:T(1,128)} %broadcast_in_dim.42), calls=%async_computation.2 | async-start | bytes 49152 | tf_op jit(solution)/shard_map/all_to_all | solution.py:128
  48.8 6.2 %all-to-all-done.2 = f32[16,1,258]{2,1,0:T(1,128)S(1)} async-done(((f32[16,1,258]{2,1,0:T(1,128)}), f32[16,1,258]{2,1,0:T(1,128)S(1)}, u32[]{:S(2)}, u32[]{:S(2)}) %all-to-all-start.2) | async-done | bytes 16544 | tf_op jit(solution)/shard_map/all_to_all | solution.py:128
  55.3 0.6 copy-done
  56.0 0.5 copy-done.1
  56.5 0.6 fusion.64
  57.3 0.6 broadcast_multiply_fusion.1
  58.2 0.3 multiply_reduce_fusion.1
  59.0 0.3 fusion.51
  59.7 10.5 %all_to_all.59 = f32[16,8,256]{2,1,0:T(8,128)S(1)} all-to-all(f32[16,8,256]{2,1,0:T(8,128)S(1)} %bitcast.37), channel_id=1, replica_groups=mesh['lines'=2,'col'=16] {'col'}, dimensions={0} | all-to-all | bytes 262144 | tf_op jit(solution)/shard_map/all_to_all | solution.py:165
  70.2 0.6 reduce_sum.153
  (55 shorter events, 3.8 us)
Async XLA Ops:
  2.0 15.3 %all-to-all-start.1 = ((f32[16,8,256]{2,1,0:T(8,128)}), f32[16,8,256]{2,1,0:T(8,128)S(1)}, u32[]{:S(2)}, u32[]{:S(2)}) async-start(f32[16,8,256]{2,1,0:T(8,128)} %broadcast_in_dim.38), calls=%async_computation.1 | async-start | bytes 262144 | tf_op jit(solution)/shard_map/all_to_all | solution.py:76
  9.4 0.7 copy-start.2
  10.7 1.3 %copy-start.3 = (f32[16]{0:T(128)S(1)}, f32[16]{0:T(128)}, u32[]{:S(2)}) copy-start(f32[16]{0:T(128)} %param.11) | copy-start | bytes 196
  12.0 0.7 copy-start.4
  17.3 13.5 %all-to-all-start = ((f32[16,2,8,256]{3,2,1,0:T(8,128)}), f32[16,2,8,256]{3,2,1,0:T(8,128)S(1)}, u32[]{:S(2)}, u32[]{:S(2)}) async-start(f32[16,2,8,256]{3,2,1,0:T(8,128)} %param.8), calls=%async_computation | async-start | bytes 524288 | tf_op jit(solution)/shard_map/all_to_all | solution.py:75
  30.8 13.5 %all-to-all-start.3 = ((f32[16,2,8,256]{3,2,1,0:T(8,128)}), f32[16,2,8,256]{3,2,1,0:T(8,128)S(1)}, u32[]{:S(2)}, u32[]{:S(2)}) async-start(f32[16,2,8,256]{3,2,1,0:T(8,128)} %param.15), calls=%async_computation.3 | async-start | bytes 524288 | tf_op jit(solution)/shard_map/all_to_all | solution.py:77
  44.9 10.0 %all-to-all-start.2 = ((f32[16,1,258]{2,1,0:T(1,128)}), f32[16,1,258]{2,1,0:T(1,128)S(1)}, u32[]{:S(2)}, u32[]{:S(2)}) async-start(f32[16,1,258]{2,1,0:T(1,128)} %broadcast_in_dim.42), calls=%async_computation.2 | async-start | bytes 49152 | tf_op jit(solution)/shard_map/all_to_all | solution.py:128
  55.2 0.7 copy-start
  55.9 0.7 copy-start.1

commit v4 on v2

--- a/solution.py
+++ b/solution.py
@@ -3,10 +3,13 @@
 import jax
 import jax.numpy as jnp
 from jax import lax
+from jax.experimental import pallas as pl
+from jax.experimental.pallas import tpu as pltpu
 from jax.sharding import Mesh
 from jax.sharding import PartitionSpec as P
 
 ITERS = 2
+INTERPRET = False
 
 
 def halo(block, axis, dim, width):
@@ -57,6 +60,123 @@
     )
     result = result + lower_face * (middle - below_cells) + upper_face * (middle - above_cells)
     return result + mass_scale * center * middle
+
+
+def edge_shifts(field):
+    rows, depth = field.shape
+    row = lax.broadcasted_iota(jnp.int32, field.shape, 0)
+    lane = lax.broadcasted_iota(jnp.int32, field.shape, 1)
+    west = jnp.where(row == 0, 0.0, pltpu.roll(field, 1, 0))
+    east = jnp.where(row == rows - 1, 0.0, pltpu.roll(field, rows - 1, 0))
+    above = jnp.where(lane == 0, 0.0, pltpu.roll(field, 1, 1))
+    below = jnp.where(lane == depth - 1, 0.0, pltpu.roll(field, depth - 1, 1))
+    return west, east, above, below
+
+
+def local_faces(center):
+    west, east, above, below = edge_shifts(center)
+    lane = lax.broadcasted_iota(jnp.int32, center.shape, 1)
+    upper = jnp.where(lane == 0, 0.0, 0.5 * (center + above))
+    return (0.5 * (center + west), 0.5 * (center + east), 0.5 * (center + below), upper, center)
+
+
+def local_stencil(field, faces_set, mass_scale):
+    west_face, east_face, lower_face, upper_face, center = faces_set
+    west, east, above, below = edge_shifts(field)
+    result = west_face * (field - west) + east_face * (field - east)
+    result = result + lower_face * (field - below) + upper_face * (field - above)
+    return result + mass_scale * center * field
+
+
+def cell_sum(field):
+    return jnp.sum(jnp.sum(field, axis=1, keepdims=True), axis=0, keepdims=True)
+
+
+def local_conjugate(source, start, operate):
+    if start is None:
+        solution = jnp.zeros_like(source)
+        residual = source
+    else:
+        solution = start
+        residual = source - operate(start)
+    direction = residual
+    norm_now = cell_sum(residual * residual)
+    for iteration in range(ITERS):
+        applied = operate(direction)
+        step_size = norm_now / cell_sum(direction * applied)
+        solution = solution + step_size * direction
+        if iteration + 1 < ITERS:
+            residual = residual - step_size * applied
+            norm_next = cell_sum(residual * residual)
+            direction = residual + (norm_next / norm_now) * direction
+            norm_now = norm_next
+    return solution
+
+
+def forward_kernel(scale_ref, primary_ref, sigma_ref, total_ref):
+    sigma = sigma_ref[...]
+    operator_faces = local_faces(sigma)
+    contrast_faces = local_faces(sigma - 1.0)
+    for field in range(primary_ref.shape[0]):
+        mass_scale = scale_ref[field]
+        primary = primary_ref[field]
+        source = -local_stencil(primary, contrast_faces, mass_scale)
+        secondary = local_conjugate(
+            source, None, lambda state: local_stencil(state, operator_faces, mass_scale)
+        )
+        total_ref[field] = primary + secondary
+
+
+def adjoint_kernel(scale_ref, charge_ref, total_ref, prior_ref, sigma_ref, gradient_ref):
+    sigma = sigma_ref[...]
+    operator_faces = local_faces(sigma)
+    lane = lax.broadcasted_iota(jnp.int32, sigma.shape, 1)
+    surface_row = (lane == 0).astype(jnp.float32)
+    gradient = jnp.zeros_like(sigma)
+    for field in range(prior_ref.shape[0]):
+        mass_scale = scale_ref[field]
+        adjoint_source = charge_ref[field] * surface_row
+        adjoint = local_conjugate(
+            adjoint_source,
+            prior_ref[field],
+            lambda state: local_stencil(state, operator_faces, mass_scale),
+        )
+        total_field = total_ref[field]
+        unused, adjoint_next, unused, adjoint_down = edge_shifts(adjoint)
+        unused, total_next, unused, total_down = edge_shifts(total_field)
+        correlation = (adjoint_next - adjoint) * (total_next - total_field)
+        correlation = correlation + (adjoint_down - adjoint) * (total_down - total_field)
+        correlation = correlation + mass_scale * adjoint * total_field
+        gradient = gradient + correlation
+    gradient_ref[...] = gradient
+
+
+def vmem_spec():
+    return pl.BlockSpec(memory_space=pltpu.MemorySpace.VMEM)
+
+
+def smem_spec():
+    return pl.BlockSpec(memory_space=pltpu.MemorySpace.SMEM)
+
+
+def forward_call(scales, primary, sigma):
+    return pl.pallas_call(
+        forward_kernel,
+        out_shape=jax.ShapeDtypeStruct(primary.shape, jnp.float32),
+        in_specs=[smem_spec(), vmem_spec(), vmem_spec()],
+        out_specs=vmem_spec(),
+        interpret=INTERPRET,
+    )(scales, primary, sigma)
+
+
+def adjoint_call(scales, charge, total_field, prior, sigma):
+    return pl.pallas_call(
+        adjoint_kernel,
+        out_shape=jax.ShapeDtypeStruct(sigma.shape, jnp.float32),
+        in_specs=[smem_spec()] + [vmem_spec()] * 4,
+        out_specs=vmem_spec(),
+        interpret=INTERPRET,
+    )(scales, charge, total_field, prior, sigma)
 
 
 def on_device(
@@ -123,8 +243,15 @@
                 norm_now = norm_next
         return solution
 
-    source = -stencil(halo(primary, "cs", 2, 1), coefficients(contrast_wide[1:-1]), mass_scale)
-    total_field = primary + conjugate(source, None)
+    scales = jnp.repeat(own_waves * own_waves, sources)
+    if spread == 1:
+        flat = (fields, width, depth)
+        total_field = forward_call(scales, primary.reshape(flat), sigma).reshape(primary.shape)
+    else:
+        source = -stencil(
+            halo(primary, "cs", 2, 1), coefficients(contrast_wide[1:-1]), mass_scale
+        )
+        total_field = primary + conjugate(source, None)
 
     surface = total_field[:, :, :, 0]
     weighted = jnp.sum(weights[:, None, None] * surface, axis=0)
@@ -152,20 +279,27 @@
         all_electrodes[:, None] == offset + jnp.arange(width)[None, :]
     ).astype(jnp.float32)
     charge_cols = jnp.sum(charge[:, :, None] * own_picks[None], axis=1)
-    surface_row = (jnp.arange(depth) == 0).astype(jnp.float32)
-    adjoint_source = weights[:, None, None, None] * charge_cols[None, :, :, None] * surface_row
-    adjoint = conjugate(adjoint_source, prior_adjoint)
-
-    adjoint_next = next_column(adjoint, "cs")
-    total_next = next_column(total_field, "cs")
-    adjoint_down = jnp.concatenate([adjoint[..., 1:], jnp.zeros_like(adjoint[..., :1])], axis=-1)
-    total_down = jnp.concatenate(
-        [total_field[..., 1:], jnp.zeros_like(total_field[..., :1])], axis=-1
-    )
-    correlation = (adjoint_next - adjoint) * (total_next - total_field)
-    correlation = correlation + (adjoint_down - adjoint) * (total_down - total_field)
-    correlation = correlation + mass_scale * adjoint * total_field
-    gradient = jnp.sum(correlation, axis=(0, 1))
+    if spread == 1:
+        charge_field = (weights[:, None, None] * charge_cols[None]).reshape(fields, width, 1)
+        gradient = adjoint_call(
+            scales, charge_field, total_field.reshape(flat), prior_adjoint.reshape(flat), sigma
+        )
+    else:
+        surface_row = (jnp.arange(depth) == 0).astype(jnp.float32)
+        adjoint_source = weights[:, None, None, None] * charge_cols[None, :, :, None] * surface_row
+        adjoint = conjugate(adjoint_source, prior_adjoint)
+        adjoint_next = next_column(adjoint, "cs")
+        total_next = next_column(total_field, "cs")
+        adjoint_down = jnp.concatenate(
+            [adjoint[..., 1:], jnp.zeros_like(adjoint[..., :1])], axis=-1
+        )
+        total_down = jnp.concatenate(
+            [total_field[..., 1:], jnp.zeros_like(total_field[..., :1])], axis=-1
+        )
+        correlation = (adjoint_next - adjoint) * (total_next - total_field)
+        correlation = correlation + (adjoint_down - adjoint) * (total_down - total_field)
+        correlation = correlation + mass_scale * adjoint * total_field
+        gradient = jnp.sum(correlation, axis=(0, 1))
     if groups > 1:
         gradient = gradient.reshape(groups, own_columns, depth)
         gradient = jnp.sum(lax.all_to_all(gradient, "kq", 0, 0, tiled=True), axis=0)

time: 58.6 us -> 65.2 us (1.11)
  blocking collectives: 10.5 us -> 22.4 us
  Pallas kernels: 0 us -> 6.94 us
  waiting for transfers between devices: 19.7 us -> 13.3 us
  starting transfers between devices: 12.1 us -> 7.41 us
  other arithmetic: 7.94 us -> 5.87 us
  local copies, waits for them, and re-layouts: 5.71 us -> 6.69 us
    all_to_all x0 -> x1, blocking collectives: none -> 11 us  [on_device(): gathered = lax.all_to_all(gathered, 'kq', 0, 0, tiled=True)]
    pallas_call x0 -> x2, Pallas kernels: none -> 6.94 us  [the longest x1 3.66 us: adjoint_call(): pl.pallas_call(adjoint_kernel, out_shape=jax.ShapeDtypeStruct(sigma.shape...]
    all_to_all x1 -> x0, waiting for transfers between devices: 6.4 us -> none  [on_device(): gathered = lax.all_to_all(gathered, 'kq', 0, 0, tiled=True)]
    all_to_all x1 -> x0, starting transfers between devices: 4.67 us -> none  [on_device(): gathered = lax.all_to_all(gathered, 'kq', 0, 0, tiled=True)]
    reduce_sum x7 -> x0, other arithmetic: 1.75 us -> none  [the longest x6 1.63 us: dots(): total = jnp.sum(left * right, axis=(2, 3))]
    mul x1, other arithmetic: 0.72 us -> 1.61 us  [on_device(): weighted = jnp.sum(weights[:, None, None] * surface, axis=0)]
    all_to_all x1, blocking collectives: 10.5 us -> 11.4 us  [on_device(): gradient = jnp.sum(lax.all_to_all(gradient, 'kq', 0, 0, tiled=True), axis=0)]
    mul x0 -> x1, local copies, waits for them, and re-layouts: none -> 0.8 us  [on_device(): weights[:, None, None] * charge_cols[None]]
  transfers between devices with their start and end apart: 2 -> 1, of which waited for: 2 -> 1; matrix products, arithmetic and copies ran while one was open for 2% -> 2% of each run, Pallas kernels for 0% -> 0%
where the time goes in v4:
time: 65.2 us; the launch traced here: 64.7 us
  blocking collectives  22.4 us (34%)
  waiting for transfers between devices  13.3 us (20%)
  starting transfers between devices  7.41 us (11%)
  Pallas kernels  6.94 us (11%)
  local copies, waits for them, and re-layouts  6.69 us (10%)
  other arithmetic  5.87 us (9%)
  between operations  2.04 us (3%)
    all_to_all x1, waiting for transfers between devices, on_device(): send = lax.all_to_all(send, 'kq', 0, 2, tiled=True)  13.3 us
    all_to_all x1, blocking collectives, on_device(): gradient = jnp.sum(lax.all_to_all(gradient, 'kq', 0, 0, tiled=True), axis=0)  11.4 us
    all_to_all x1, blocking collectives, on_device(): gathered = lax.all_to_all(gathered, 'kq', 0, 0, tiled=True)  11 us
    all_to_all x1, starting transfers between devices, on_device(): send = lax.all_to_all(send, 'kq', 0, 2, tiled=True)  7.41 us
    pallas_call x1, Pallas kernels, adjoint_call(): pl.pallas_call(adjoint_kernel, out_shape=jax.ShapeDtypeStruct(sigma.shape...  3.66 us
    pallas_call x1, Pallas kernels, forward_call(): pl.pallas_call(forward_kernel, out_shape=jax.ShapeDtypeStruct(primary.sha...  3.27 us
    concatenate x1, other arithmetic, on_device(): jnp.concatenate([by_group(primary), by_group(prior_adjoint), sigma_copies...  1.93 us
    unnamed x11, local copies, waits for them, and re-layouts  1.82 us
  transfers between devices with their start and end apart: 1, of which 1 were waited for; matrix products, arithmetic and copies ran while one was open for 2% of the time, Pallas kernels for 0%

profile of v4, /device:TPU:0, one launch (start us, length us, event | category | flops | bytes accessed | tf_op | source)
XLA Modules:
  0.0 64.7 jit_solution(6340074078849353918)
XLA Ops:
  0.6 0.7 %broadcast_in_dim.4 = f32[16,1,8,256]{3,2,1,0:T(8,128)S(1)} broadcast(f32[8,256]{1,0:T(8,128)} %param.9), dimensions={2,3} | broadcast | bytes 139264 | tf_op jit(solution)/shard_map/broadcast_in_dim | solution.py:196
  1.3 1.9 %pad_maximum_fusion = f32[16,5,8,256]{3,2,1,0:T(8,128)} fusion(f32[16,1,8,256]{3,2,1,0:T(8,128)S(1)} %broadcast_in_dim.4, f32[16,2,8,256]{3,2,1,0:T(8,128)} %param.15, f32[16,2,8,256]{3,2,1,0:T(8,128)} %param.8), kind=kLoop, calls=%fused_computation | loop fusion | flops 327680 | bytes 1310720 | tf_op jit(solution)/shard_map/concatenate | solution.py:197
  3.3 7.4 %all-to-all-start = ((f32[16,5,8,256]{3,2,1,0:T(8,128)}), f32[16,5,8,256]{3,2,1,0:T(8,128)S(1)}, u32[]{:S(2)}, u32[]{:S(2)}) async-start(f32[16,5,8,256]{3,2,1,0:T(8,128)} %pad_maximum_fusion), calls=%async_computation | async-start | bytes 1310720 | tf_op jit(solution)/shard_map/all_to_all | solution.py:199
  10.7 0.6 copy-done.2
  11.4 0.6 dynamic_slice.6
  12.0 0.6 dynamic_slice.7
  13.9 13.3 %all-to-all-done = f32[16,5,8,256]{3,2,1,0:T(8,128)S(1)} async-done(((f32[16,5,8,256]{3,2,1,0:T(8,128)}), f32[16,5,8,256]{3,2,1,0:T(8,128)S(1)}, u32[]{:S(2)}, u32[]{:S(2)}) %all-to-all-start) | async-done | bytes 655392 | tf_op jit(solution)/shard_map/all_to_all | solution.py:199
  27.3 0.7 %slice_bitcast_fusion.sigma_ref = f32[128,256]{1,0:T(8,128)} fusion(f32[1,5,16,8,256]{4,3,1,2,0:T(8,128)S(1)} %bitcast.20), kind=kLoop, calls=%fused_computation.5 | loop fusion | bytes 262144 | tf_op jit(solution)/shard_map/squeeze | solution.py:204
  28.0 0.9 %copy_bitcast_fusion = (f32[2,128,256]{2,1,0:T(8,128)}, f32[2,128,256]{2,1,0:T(8,128)}) fusion(f32[1,2,16,8,256]{4,3,1,2,0:T(8,128)S(1)} %get-tuple-element.4, f32[1,2,16,8,256]{4,3,1,2,0:T(8,128)S(1)} %get-tuple-element.5), kind=kLoop, calls=%fused_computation.1 | loop fusion | bytes 1048576 | tf_op jit(solution)/shard_map/slice | solution.py:203
  28.8 0.5 reshape.113.scale_ref
  29.3 3.3 %shard_map.95.total_ref = f32[2,128,256]{2,1,0:T(8,128)} custom-call(f32[2]{0:T(128)} %reshape.113.scale_ref, f32[2,128,256]{2,1,0:T(8,128)} %get-tuple-element.7.primary_ref, f32[128,256]{1,0:T(8,128)} %slice_bitcast_fusion.sigma_ref), custom_call_target="tpu_custom_call" | custom-call | tf_op jit(solution)/shard_map/pallas_call | solution.py:163
  32.6 1.6 %fusion = f32[2,128]{1,0:T(2,128)S(1)} fusion(f32[1,2,128,256]{3,2,1,0:T(8,128)} %bitcast.22, f32[]{:T(128)} %bitcast), kind=kLoop, calls=%fused_computation.4 | loop fusion | flops 256 | bytes 2052 | tf_op jit(solution)/shard_map/mul | solution.py:257
  34.3 11.0 %all_to_all.29 = f32[16,1,258]{2,1,0:T(1,128)S(1)} all-to-all(f32[16,1,258]{2,1,0:T(1,128)S(1)} %broadcast_in_dim.5), channel_id=1, replica_groups=mesh['lines'=2,'col'=16] {'col'}, dimensions={0} | all-to-all | bytes 33024 | tf_op jit(solution)/shard_map/all_to_all | solution.py:261
  45.6 0.6 copy-done
  46.2 0.2 select_reduce_fusion.1
  46.3 0.5 copy-done.1
  46.9 0.6 fusion.2
  47.4 0.1 select_reduce_fusion
  47.5 0.1 multiply_reduce_fusion
  47.6 0.6 multiply_bitcast_fusion
  48.3 0.8 %copy.20.charge_ref = f32[2,128,1]{2,1,0:T(8,128)} copy(f32[2,128,1]{1,0,2:T(2,128)S(1)} %multiply_bitcast_fusion) | data formatting | bytes 2048 | tf_op jit(solution)/shard_map/mul | solution.py:283
  49.0 3.7 %shard_map.96 = f32[128,256]{1,0:T(8,128)} custom-call(f32[2]{0:T(128)} %reshape.113.scale_ref, f32[2,128,1]{2,1,0:T(8,128)} %copy.20.charge_ref, f32[2,128,256]{2,1,0:T(8,128)} %shard_map.95.total_ref, f32[2,128,256]{2,1,0:T(8,128)} %get-tuple-element.6.prior_ref, f32[128,256]{1,0:T(8,128)} %slice_bitcast_fusion.sigma_ref), custom_call_target="tpu_custom_call" | custom-call | tf_op jit(solution)/shard_map/pallas_call | solution.py:173
  52.7 11.4 %all_to_all.30 = f32[16,8,256]{2,1,0:T(8,128)S(1)} all-to-all(f32[16,8,256]{2,1,0:T(8,128)} %bitcast.23), channel_id=1, replica_groups=mesh['lines'=2,'col'=16] {'col'}, dimensions={0} | all-to-all | bytes 262144 | tf_op jit(solution)/shard_map/all_to_all | solution.py:305
  64.1 0.6 reduce_sum.63
  (18 shorter events, 0.4 us)
Async XLA Ops:
  3.3 24.0 %all-to-all-start = ((f32[16,5,8,256]{3,2,1,0:T(8,128)}), f32[16,5,8,256]{3,2,1,0:T(8,128)S(1)}, u32[]{:S(2)}, u32[]{:S(2)}) async-start(f32[16,5,8,256]{3,2,1,0:T(8,128)} %pad_maximum_fusion), calls=%async_computation | async-start | bytes 1310720 | tf_op jit(solution)/shard_map/all_to_all | solution.py:199
  10.7 0.7 %copy-start.2 = (f32[16]{0:T(128)S(1)}, f32[16]{0:T(128)}, u32[]{:S(2)}) copy-start(f32[16]{0:T(128)} %param.11) | copy-start | bytes 196
  11.4 0.7 %copy-start.3 = (f32[16]{0:T(128)S(1)}, f32[16]{0:T(128)}, u32[]{:S(2)}) copy-start(f32[16]{0:T(128)} %param.10) | copy-start | bytes 196
  12.6 1.3 %copy-start.4 = (s32[2]{0:T(128)S(1)}, s32[2]{0:T(128)}, u32[]{:S(2)}) copy-start(s32[2]{0:T(128)} %param.12) | copy-start | bytes 28
  45.5 0.7 %copy-start = (s32[2,32]{1,0:T(2,128)S(1)}, s32[2,32]{1,0:T(2,128)}, u32[]{:S(2)}) copy-start(s32[2,32]{1,0:T(2,128)} %param.13) | copy-start | bytes 772
  46.2 0.7 %copy-start.1 = (f32[2,32]{1,0:T(2,128)S(1)}, f32[2,32]{1,0:T(2,128)}, u32[]{:S(2)}) copy-start(f32[2,32]{1,0:T(2,128)} %param.14) | copy-start | bytes 772

commit v5 on v2

--- a/solution.py
+++ b/solution.py
@@ -3,10 +3,13 @@
 import jax
 import jax.numpy as jnp
 from jax import lax
+from jax.experimental import pallas as pl
+from jax.experimental.pallas import tpu as pltpu
 from jax.sharding import Mesh
 from jax.sharding import PartitionSpec as P
 
 ITERS = 2
+INTERPRET = False
 
 
 def halo(block, axis, dim, width):
@@ -59,6 +62,37 @@
     return result + mass_scale * center * middle
 
 
+def pack_kernel(primary_ref, prior_ref, sigma_ref, send_ref, flags):
+    groups, fields = primary_ref.shape[:2]
+    copies = [
+        pltpu.make_async_copy(primary_ref, send_ref.at[:, 0:fields], flags.at[0]),
+        pltpu.make_async_copy(prior_ref, send_ref.at[:, fields : 2 * fields], flags.at[1]),
+    ]
+    for target in range(groups):
+        copies.append(
+            pltpu.make_async_copy(
+                sigma_ref, send_ref.at[target, 2 * fields], flags.at[2 + target]
+            )
+        )
+    for copy in copies:
+        copy.start()
+    for copy in copies:
+        copy.wait()
+
+
+def pack(primary, prior, sigma):
+    groups, fields, rows, depth = primary.shape
+    anywhere = pl.BlockSpec(memory_space=pl.ANY)
+    return pl.pallas_call(
+        pack_kernel,
+        out_shape=jax.ShapeDtypeStruct((groups, 2 * fields + 1, rows, depth), jnp.float32),
+        in_specs=[anywhere] * 3,
+        out_specs=anywhere,
+        scratch_shapes=[pltpu.SemaphoreType.DMA((groups + 2,))],
+        interpret=INTERPRET,
+    )(primary, prior, sigma)
+
+
 def on_device(
     primary, conductivity, wavenumbers, quadrature, electrodes, far_pole, observed, prior_adjoint
 ):
@@ -73,8 +107,7 @@
     def by_group(array):
         return array.reshape(groups, fields, own_columns, depth)
 
-    sigma_copies = jnp.broadcast_to(conductivity[None, None], (groups, 1, own_columns, depth))
-    send = jnp.concatenate([by_group(primary), by_group(prior_adjoint), sigma_copies], axis=1)
+    send = pack(by_group(primary), by_group(prior_adjoint), conductivity)
     if groups > 1:
         send = lax.all_to_all(send, "kq", 0, 2, tiled=True)
     received = send[0]

time: 58.6 us -> 77 us (1.31)
  Pallas kernels: 0 us -> 21.1 us
  other arithmetic: 7.94 us -> 6.02 us
    pallas_call x0 -> x1, Pallas kernels: none -> 21.1 us  [pack(): pl.pallas_call(pack_kernel, out_shape=jax.ShapeDtypeStruct((groups, 2 * f...]
    concatenate x1 -> x0, other arithmetic: 1.93 us -> none  [on_device(): jnp.concatenate([by_group(primary), by_group(prior_adjoint), sigma_copies...]
where the time goes in v5:
time: 77 us; the launch traced here: 76.6 us
  Pallas kernels  21.1 us (27%)
  waiting for transfers between devices  19.6 us (25%)
  starting transfers between devices  12.1 us (16%)
  blocking collectives  10.5 us (14%)
  other arithmetic  6.02 us (8%)
  local copies, waits for them, and re-layouts  5.07 us (7%)
  between operations  2.24 us (3%)
    pallas_call x1, Pallas kernels, pack(): pl.pallas_call(pack_kernel, out_shape=jax.ShapeDtypeStruct((groups, 2 * f...  21.1 us
    all_to_all x1, waiting for transfers between devices, on_device(): send = lax.all_to_all(send, 'kq', 0, 2, tiled=True)  13.3 us
    all_to_all x1, blocking collectives, on_device(): gradient = jnp.sum(lax.all_to_all(gradient, 'kq', 0, 0, tiled=True), axis=0)  10.5 us
    all_to_all x1, starting transfers between devices, on_device(): send = lax.all_to_all(send, 'kq', 0, 2, tiled=True)  7.43 us
    all_to_all x1, waiting for transfers between devices, on_device(): gathered = lax.all_to_all(gathered, 'kq', 0, 0, tiled=True)  6.27 us
    all_to_all x1, starting transfers between devices, on_device(): gathered = lax.all_to_all(gathered, 'kq', 0, 0, tiled=True)  4.67 us
    unnamed x11, local copies, waits for them, and re-layouts  1.83 us
    reduce_sum x6, other arithmetic, dots(): total = jnp.sum(left * right, axis=(2, 3))  1.63 us
  transfers between devices with their start and end apart: 2, of which 2 were waited for; matrix products, arithmetic and copies ran while one was open for 2% of the time, Pallas kernels for 0%

profile of v5, /device:TPU:0, one launch (start us, length us, event | category | flops | bytes accessed | tf_op | source)
XLA Modules:
  0.0 76.6 jit_solution(13445857406918674878)
XLA Ops:
  0.6 21.1 %shard_map.95 = f32[16,5,8,256]{3,2,1,0:T(8,128)} custom-call(f32[16,2,8,256]{3,2,1,0:T(8,128)} %primary_ref.1, f32[16,2,8,256]{3,2,1,0:T(8,128)} %prior_ref.1, f32[8,256]{1,0:T(8,128)} %sigma_ref.1), custom_call_target="tpu_custom_call" | custom-call | tf_op jit(solution)/shard_map/pallas_call | solution.py:86
  21.8 7.4 %all-to-all-start = ((f32[16,5,8,256]{3,2,1,0:T(8,128)}), f32[16,5,8,256]{3,2,1,0:T(8,128)S(1)}, u32[]{:S(2)}, u32[]{:S(2)}) async-start(f32[16,5,8,256]{3,2,1,0:T(8,128)} %shard_map.95), calls=%async_computation | async-start | bytes 1310720 | tf_op jit(solution)/shard_map/all_to_all | solution.py:112
  29.2 0.6 copy-done.2
  29.9 0.6 dynamic_slice.7
  31.8 0.6 dynamic_slice.6
  32.4 13.3 %all-to-all-done = f32[16,5,8,256]{3,2,1,0:T(8,128)S(1)} async-done(((f32[16,5,8,256]{3,2,1,0:T(8,128)}), f32[16,5,8,256]{3,2,1,0:T(8,128)S(1)}, u32[]{:S(2)}, u32[]{:S(2)}) %all-to-all-start) | async-done | bytes 655392 | tf_op jit(solution)/shard_map/all_to_all | solution.py:112
  46.5 0.2 fusion.66
  46.9 0.3 multiply_reduce_fusion.4
  47.2 0.2 multiply_reduce_fusion.3
  47.7 0.3 fusion.52
  48.1 0.7 fusion.58
  48.9 0.6 broadcast_in_dim.39
  49.5 4.7 %all-to-all-start.1 = ((f32[16,1,258]{2,1,0:T(1,128)}), f32[16,1,258]{2,1,0:T(1,128)S(1)}, u32[]{:S(2)}, u32[]{:S(2)}) async-start(f32[16,1,258]{2,1,0:T(1,128)} %broadcast_in_dim.39), calls=%async_computation.1 | async-start | bytes 49152 | tf_op jit(solution)/shard_map/all_to_all | solution.py:167
  54.5 6.3 %all-to-all-done.1 = f32[16,1,258]{2,1,0:T(1,128)S(1)} async-done(((f32[16,1,258]{2,1,0:T(1,128)}), f32[16,1,258]{2,1,0:T(1,128)S(1)}, u32[]{:S(2)}, u32[]{:S(2)}) %all-to-all-start.1) | async-done | bytes 16544 | tf_op jit(solution)/shard_map/all_to_all | solution.py:167
  61.0 0.6 copy-done
  61.8 0.5 copy-done.1
  62.3 0.6 fusion.64
  63.0 0.6 broadcast_multiply_fusion.1
  63.7 0.2 fusion.31
  64.0 0.3 multiply_reduce_fusion.1
  64.3 0.2 multiply_reduce_fusion
  64.8 0.3 fusion.51
  65.5 10.5 %all_to_all.29 = f32[16,8,256]{2,1,0:T(8,128)S(1)} all-to-all(f32[16,8,256]{2,1,0:T(8,128)S(1)} %bitcast.30), channel_id=1, replica_groups=mesh['lines'=2,'col'=16] {'col'}, dimensions={0} | all-to-all | bytes 262144 | tf_op jit(solution)/shard_map/all_to_all | solution.py:204
  76.0 0.6 reduce_sum.153
  (52 shorter events, 3.0 us)
Async XLA Ops:
  21.8 24.0 %all-to-all-start = ((f32[16,5,8,256]{3,2,1,0:T(8,128)}), f32[16,5,8,256]{3,2,1,0:T(8,128)S(1)}, u32[]{:S(2)}, u32[]{:S(2)}) async-start(f32[16,5,8,256]{3,2,1,0:T(8,128)} %shard_map.95), calls=%async_computation | async-start | bytes 1310720 | tf_op jit(solution)/shard_map/all_to_all | solution.py:112
  29.2 0.7 copy-start.2
  30.4 1.3 %copy-start.3 = (f32[16]{0:T(128)S(1)}, f32[16]{0:T(128)}, u32[]{:S(2)}) copy-start(f32[16]{0:T(128)} %param.11) | copy-start | bytes 196
  31.8 0.7 copy-start.4
  49.5 11.2 %all-to-all-start.1 = ((f32[16,1,258]{2,1,0:T(1,128)}), f32[16,1,258]{2,1,0:T(1,128)S(1)}, u32[]{:S(2)}, u32[]{:S(2)}) async-start(f32[16,1,258]{2,1,0:T(1,128)} %broadcast_in_dim.39), calls=%async_computation.1 | async-start | bytes 49152 | tf_op jit(solution)/shard_map/all_to_all | solution.py:167
  60.9 0.7 copy-start
  61.6 0.7 copy-start.1

commit v6 on v2

--- a/solution.py
+++ b/solution.py
@@ -3,6 +3,8 @@
 import jax
 import jax.numpy as jnp
 from jax import lax
+from jax.experimental import pallas as pl
+from jax.experimental.pallas import tpu as pltpu
 from jax.sharding import Mesh
 from jax.sharding import PartitionSpec as P
 
@@ -59,6 +61,26 @@
     return result + mass_scale * center * middle
 
 
+def pack_kernel(primary_ref, prior_ref, sigma_ref, send_ref):
+    fields = primary_ref.shape[1]
+    send_ref[:, 0:fields] = primary_ref[...]
+    send_ref[:, fields : 2 * fields] = prior_ref[...]
+    sigma = sigma_ref[...]
+    for target in range(send_ref.shape[0]):
+        send_ref[target, 2 * fields] = sigma
+
+
+def pack(primary, prior, sigma):
+    groups, fields, rows, depth = primary.shape
+    vmem = pl.BlockSpec(memory_space=pltpu.MemorySpace.VMEM)
+    return pl.pallas_call(
+        pack_kernel,
+        out_shape=jax.ShapeDtypeStruct((groups, 2 * fields + 1, rows, depth), jnp.float32),
+        in_specs=[vmem] * 3,
+        out_specs=vmem,
+    )(primary, prior, sigma)
+
+
 def on_device(
     primary, conductivity, wavenumbers, quadrature, electrodes, far_pole, observed, prior_adjoint
 ):
@@ -73,8 +95,7 @@
     def by_group(array):
         return array.reshape(groups, fields, own_columns, depth)
 
-    sigma_copies = jnp.broadcast_to(conductivity[None, None], (groups, 1, own_columns, depth))
-    send = jnp.concatenate([by_group(primary), by_group(prior_adjoint), sigma_copies], axis=1)
+    send = pack(by_group(primary), by_group(prior_adjoint), conductivity)
     if groups > 1:
         send = lax.all_to_all(send, "kq", 0, 2, tiled=True)
     received = send[0]
@@ -129,6 +150,8 @@
     surface = total_field[:, :, :, 0]
     weighted = jnp.sum(weights[:, None, None] * surface, axis=0)
     packet = jnp.concatenate([weighted.reshape(-1), electrodes.astype(jnp.float32)])
+    pole_hits = (far_pole[:, :, None] == jnp.arange(far_pole.shape[1])[None, None, :]).astype(jnp.float32)
+    packet, pole_hits, observed = lax.optimization_barrier((packet, pole_hits, observed))
     gathered = jnp.broadcast_to(packet[None], (groups,) + packet.shape)
     if groups > 1:
         gathered = lax.all_to_all(gathered, "kq", 0, 0, tiled=True)
@@ -142,7 +165,6 @@
 
     picks = (all_electrodes[:, None] == jnp.arange(columns)[None, :]).astype(jnp.float32)
     potentials = jnp.sum(line_surface[:, None, :] * picks[None], axis=2)
-    pole_hits = (far_pole[:, :, None] == jnp.arange(count)[None, None, :]).astype(jnp.float32)
     far_potentials = jnp.sum(potentials[:, None, :] * pole_hits, axis=2)
     predicted = potentials - far_potentials
     misfit = predicted - observed

time: 58.6 us -> 57.2 us (0.976)
  Pallas kernels: 0 us -> 1.91 us
  other arithmetic: 7.94 us -> 6.04 us
  waiting for transfers between devices: 19.7 us -> 18.8 us
    concatenate x1 -> x0, other arithmetic: 1.93 us -> none  [on_device(): jnp.concatenate([by_group(primary), by_group(prior_adjoint), sigma_copies...]
    pallas_call x0 -> x1, Pallas kernels: none -> 1.91 us  [pack(): pl.pallas_call(pack_kernel, out_shape=jax.ShapeDtypeStruct((groups, 2 * f...]
    all_to_all x1, waiting for transfers between devices: 13.3 us -> 12.6 us  [on_device(): send = lax.all_to_all(send, 'kq', 0, 2, tiled=True)]
    broadcast_in_dim x1 -> x0, local copies, waits for them, and re-layouts: 0.71 us -> none  [on_device(): jnp.broadcast_to(conductivity[None, None], (groups, 1, own_columns, depth))]
  transfers between devices with their start and end apart: 2 -> 2, of which waited for: 2 -> 2; matrix products, arithmetic and copies ran while one was open for 2% -> 3% of each run, Pallas kernels for 0% -> 0%
where the time goes in v6:
time: 57.2 us; the launch traced here: 56.8 us
  waiting for transfers between devices  18.8 us (33%)
  starting transfers between devices  12.1 us (21%)
  blocking collectives  10.5 us (18%)
  other arithmetic  6.04 us (11%)
  local copies, waits for them, and re-layouts  5.21 us (9%)
  between operations  2.24 us (4%)
  Pallas kernels  1.91 us (3%)
    all_to_all x1, waiting for transfers between devices, on_device(): send = lax.all_to_all(send, 'kq', 0, 2, tiled=True)  12.6 us
    all_to_all x1, blocking collectives, on_device(): gradient = jnp.sum(lax.all_to_all(gradient, 'kq', 0, 0, tiled=True), axis=0)  10.5 us
    all_to_all x1, starting transfers between devices, on_device(): send = lax.all_to_all(send, 'kq', 0, 2, tiled=True)  7.41 us
    all_to_all x1, waiting for transfers between devices, on_device(): gathered = lax.all_to_all(gathered, 'kq', 0, 0, tiled=True)  6.27 us
    all_to_all x1, starting transfers between devices, on_device(): gathered = lax.all_to_all(gathered, 'kq', 0, 0, tiled=True)  4.67 us
    unnamed x11, local copies, waits for them, and re-layouts  1.96 us
    pallas_call x1, Pallas kernels, pack(): pl.pallas_call(pack_kernel, out_shape=jax.ShapeDtypeStruct((groups, 2 * f...  1.91 us
    reduce_sum x6, other arithmetic, dots(): total = jnp.sum(left * right, axis=(2, 3))  1.63 us
  transfers between devices with their start and end apart: 2, of which 2 were waited for; matrix products, arithmetic and copies ran while one was open for 3% of the time, Pallas kernels for 0%

profile of v6, /device:TPU:0, one launch (start us, length us, event | category | flops | bytes accessed | tf_op | source)
XLA Modules:
  0.0 56.8 jit_solution(11863043105502098699)
XLA Ops:
  0.6 1.9 %shard_map.95 = f32[16,5,8,256]{3,2,1,0:T(8,128)} custom-call(f32[16,2,8,256]{3,2,1,0:T(8,128)} %primary_ref.1, f32[16,2,8,256]{3,2,1,0:T(8,128)} %prior_ref.1, f32[8,256]{1,0:T(8,128)} %sigma_ref.1), custom_call_target="tpu_custom_call" | custom-call | tf_op jit(solution)/shard_map/pallas_call | solution.py:76
  2.5 7.4 %all-to-all-start = ((f32[16,5,8,256]{3,2,1,0:T(8,128)}), f32[16,5,8,256]{3,2,1,0:T(8,128)S(1)}, u32[]{:S(2)}, u32[]{:S(2)}) async-start(f32[16,5,8,256]{3,2,1,0:T(8,128)} %shard_map.95), calls=%async_computation | async-start | bytes 1310720 | tf_op jit(solution)/shard_map/all_to_all | solution.py:100
  10.0 0.6 %copy-done.2 = f32[16]{0:T(128)S(1)} copy-done((f32[16]{0:T(128)S(1)}, f32[16]{0:T(128)}, u32[]{:S(2)}) %copy-start.2) | copy-done | bytes 88
  10.6 0.6 %dynamic_slice.7 = f32[1]{0:T(128)} dynamic-slice(f32[16]{0:T(128)S(1)} %copy-done.2, s32[]{:T(128)S(6)} %select_n.15), dynamic_slice_sizes={1} | dynamic-slice | bytes 12 | tf_op jit(solution)/shard_map/dynamic_slice | solution.py:113
  12.5 0.6 %dynamic_slice.6 = f32[1]{0:T(128)} dynamic-slice(f32[16]{0:T(128)S(1)} %copy-done.3, s32[]{:T(128)S(6)} %select_n.15), dynamic_slice_sizes={1} | dynamic-slice | bytes 12 | tf_op jit(solution)/shard_map/dynamic_slice | solution.py:114
  13.2 0.7 %copy-done = s32[2,32]{1,0:T(2,128)S(1)} copy-done((s32[2,32]{1,0:T(2,128)S(1)}, s32[2,32]{1,0:T(2,128)}, u32[]{:S(2)}) %copy-start) | copy-done | bytes 280
  14.0 12.6 %all-to-all-done = f32[16,5,8,256]{3,2,1,0:T(8,128)S(1)} async-done(((f32[16,5,8,256]{3,2,1,0:T(8,128)}), f32[16,5,8,256]{3,2,1,0:T(8,128)S(1)}, u32[]{:S(2)}, u32[]{:S(2)}) %all-to-all-start) | async-done | bytes 655392 | tf_op jit(solution)/shard_map/all_to_all | solution.py:100
  27.3 0.2 fusion.67
  27.6 0.3 multiply_reduce_fusion.4
  28.0 0.2 multiply_reduce_fusion.3
  28.5 0.3 fusion.52
  28.9 0.7 %fusion.58 = f32[2,128]{1,0:T(2,128)S(1)} fusion(f32[1,2,128,256]{3,2,1,0:T(8,128)S(1)} %add_add_fusion, f32[]{:T(128)} %bitcast), kind=kLoop, calls=%fused_computation.89 | loop fusion | flops 256 | bytes 2052 | tf_op jit(solution)/shard_map/mul | solution.py:151
  29.6 0.6 %broadcast_in_dim.39 = f32[16,1,258]{2,1,0:T(1,128)} broadcast(f32[258]{0:T(512)S(1)} %pad_maximum_fusion), dimensions={2} | broadcast | bytes 17544 | tf_op jit(solution)/shard_map/broadcast_in_dim | solution.py:155
  30.2 4.7 %all-to-all-start.1 = ((f32[16,1,258]{2,1,0:T(1,128)}), f32[16,1,258]{2,1,0:T(1,128)S(1)}, u32[]{:S(2)}, u32[]{:S(2)}) async-start(f32[16,1,258]{2,1,0:T(1,128)} %broadcast_in_dim.39), calls=%async_computation.1 | async-start | bytes 49152 | tf_op jit(solution)/shard_map/all_to_all | solution.py:157
  35.2 6.3 %all-to-all-done.1 = f32[16,1,258]{2,1,0:T(1,128)S(1)} async-done(((f32[16,1,258]{2,1,0:T(1,128)}), f32[16,1,258]{2,1,0:T(1,128)S(1)}, u32[]{:S(2)}, u32[]{:S(2)}) %all-to-all-start.1) | async-done | bytes 16544 | tf_op jit(solution)/shard_map/all_to_all | solution.py:157
  41.9 0.6 %copy-done.1 = f32[2,32]{1,0:T(2,128)S(1)} copy-done((f32[2,32]{1,0:T(2,128)S(1)}, f32[2,32]{1,0:T(2,128)}, u32[]{:S(2)}) %copy-start.1) | copy-done | bytes 280
  42.5 0.6 fusion.65
  43.2 0.6 %broadcast_multiply_fusion.1 = f32[2,128]{1,0:T(2,128)S(1)} fusion(f32[2,128]{1,0:T(2,128)S(1)} %multiply_reduce_fusion.6, f32[]{:T(128)} %bitcast), kind=kLoop, calls=%fused_computation.115 | loop fusion | flops 256 | bytes 2052 | tf_op jit(solution)/shard_map/mul | solution.py:178
  43.9 0.2 fusion.31
  44.2 0.3 multiply_reduce_fusion.1
  44.5 0.2 multiply_reduce_fusion
  45.0 0.3 fusion.51
  45.7 10.5 %all_to_all.29 = f32[16,8,256]{2,1,0:T(8,128)S(1)} all-to-all(f32[16,8,256]{2,1,0:T(8,128)S(1)} %bitcast.30), channel_id=1, replica_groups=mesh['lines'=2,'col'=16] {'col'}, dimensions={0} | all-to-all | bytes 262144 | tf_op jit(solution)/shard_map/all_to_all | solution.py:193
  56.2 0.6 %reduce_sum.153 = f32[8,256]{1,0:T(8,128)} reduce(f32[16,8,256]{2,1,0:T(8,128)S(1)} %all_to_all.29, f32[]{:T(128)} %constant.13.clone.1), dimensions={0}, to_apply=%region_14.15 | reduce | flops 30720 | bytes 139268 | tf_op jit(solution)/shard_map/reduce_sum | solution.py:193
  (53 shorter events, 3.0 us)
Async XLA Ops:
  2.5 24.0 %all-to-all-start = ((f32[16,5,8,256]{3,2,1,0:T(8,128)}), f32[16,5,8,256]{3,2,1,0:T(8,128)S(1)}, u32[]{:S(2)}, u32[]{:S(2)}) async-start(f32[16,5,8,256]{3,2,1,0:T(8,128)} %shard_map.95), calls=%async_computation | async-start | bytes 1310720 | tf_op jit(solution)/shard_map/all_to_all | solution.py:100
  10.0 0.7 %copy-start.2 = (f32[16]{0:T(128)S(1)}, f32[16]{0:T(128)}, u32[]{:S(2)}) copy-start(f32[16]{0:T(128)} %param.10) | copy-start | bytes 196
  11.2 1.3 %copy-start.3 = (f32[16]{0:T(128)S(1)}, f32[16]{0:T(128)}, u32[]{:S(2)}) copy-start(f32[16]{0:T(128)} %param.11) | copy-start | bytes 196
  12.5 0.7 %copy-start.4 = (s32[2]{0:T(128)S(1)}, s32[2]{0:T(128)}, u32[]{:S(2)}) copy-start(s32[2]{0:T(128)} %param.12) | copy-start | bytes 28
  13.2 0.7 %copy-start = (s32[2,32]{1,0:T(2,128)S(1)}, s32[2,32]{1,0:T(2,128)}, u32[]{:S(2)}) copy-start(s32[2,32]{1,0:T(2,128)} %param.13) | copy-start | bytes 772
  30.2 11.2 %all-to-all-start.1 = ((f32[16,1,258]{2,1,0:T(1,128)}), f32[16,1,258]{2,1,0:T(1,128)S(1)}, u32[]{:S(2)}, u32[]{:S(2)}) async-start(f32[16,1,258]{2,1,0:T(1,128)} %broadcast_in_dim.39), calls=%async_computation.1 | async-start | bytes 49152 | tf_op jit(solution)/shard_map/all_to_all | solution.py:157
  41.8 0.7 %copy-start.1 = (f32[2,32]{1,0:T(2,128)S(1)}, f32[2,32]{1,0:T(2,128)}, u32[]{:S(2)}) copy-start(f32[2,32]{1,0:T(2,128)} %param.14) | copy-start | bytes 772

commit v7 on v6

--- a/solution.py
+++ b/solution.py
@@ -9,6 +9,7 @@
 from jax.sharding import PartitionSpec as P
 
 ITERS = 2
+INTERPRET = False
 
 
 def halo(block, axis, dim, width):
@@ -72,14 +73,17 @@
 
 def pack(primary, prior, sigma):
     groups, fields, rows, depth = primary.shape
-    vmem = pl.BlockSpec(memory_space=pltpu.MemorySpace.VMEM)
+    steps = 2 if groups % 2 == 0 else 1
+    chunk = groups // steps
+    part = pl.BlockSpec((chunk, fields, rows, depth), lambda i: (i, 0, 0, 0))
     return pl.pallas_call(
         pack_kernel,
         out_shape=jax.ShapeDtypeStruct((groups, 2 * fields + 1, rows, depth), jnp.float32),
-        in_specs=[vmem] * 3,
-        out_specs=vmem,
+        grid=(steps,),
+        in_specs=[part, part, pl.BlockSpec((rows, depth), lambda i: (0, 0))],
+        out_specs=pl.BlockSpec((chunk, 2 * fields + 1, rows, depth), lambda i: (i, 0, 0, 0)),
+        interpret=INTERPRET,
     )(primary, prior, sigma)
-
 
 def on_device(
     primary, conductivity, wavenumbers, quadrature, electrodes, far_pole, observed, prior_adjoint
@@ -151,10 +155,10 @@
     weighted = jnp.sum(weights[:, None, None] * surface, axis=0)
     packet = jnp.concatenate([weighted.reshape(-1), electrodes.astype(jnp.float32)])
     pole_hits = (far_pole[:, :, None] == jnp.arange(far_pole.shape[1])[None, None, :]).astype(jnp.float32)
-    packet, pole_hits, observed = lax.optimization_barrier((packet, pole_hits, observed))
+    packet, pole_hits, held = lax.optimization_barrier((packet, pole_hits, 0.0 - observed))
     gathered = jnp.broadcast_to(packet[None], (groups,) + packet.shape)
     if groups > 1:
-        gathered = lax.all_to_all(gathered, "kq", 0, 0, tiled=True)
+        gathered = lax.all_to_all(gathered, "kq", 0, 0)
     if spread > 1:
         gathered = lax.all_gather(gathered, "cs")
     gathered = gathered.reshape(spread * groups, -1)
@@ -167,7 +171,7 @@
     potentials = jnp.sum(line_surface[:, None, :] * picks[None], axis=2)
     far_potentials = jnp.sum(potentials[:, None, :] * pole_hits, axis=2)
     predicted = potentials - far_potentials
-    misfit = predicted - observed
+    misfit = predicted + held
     returned = jnp.sum(misfit[:, :, None] * pole_hits, axis=1)
     charge = misfit - returned
     own_picks = (

time: 57.2 us -> 56.6 us (0.990)
  waiting for transfers between devices: 18.8 us -> 18.2 us
    all_to_all x1, waiting for transfers between devices: 12.6 us -> 11.9 us  [on_device(): send = lax.all_to_all(send, 'kq', 0, 2, tiled=True)]
    add x0 -> x1, other arithmetic: none -> 0.58 us  [on_device(): misfit = predicted + held]
where the time goes in v7:
time: 56.6 us; the launch traced here: 56.2 us
  waiting for transfers between devices  18.2 us (32%)
  starting transfers between devices  12.1 us (21%)
  blocking collectives  10.5 us (19%)
  other arithmetic  6.06 us (11%)
  local copies, waits for them, and re-layouts  5.29 us (9%)
  between operations  2.24 us (4%)
  Pallas kernels  1.88 us (3%)
    all_to_all x1, waiting for transfers between devices, on_device(): send = lax.all_to_all(send, 'kq', 0, 2, tiled=True)  11.9 us
    all_to_all x1, blocking collectives, on_device(): gradient = jnp.sum(lax.all_to_all(gradient, 'kq', 0, 0, tiled=True), axis=0)  10.5 us
    all_to_all x1, starting transfers between devices, on_device(): send = lax.all_to_all(send, 'kq', 0, 2, tiled=True)  7.41 us
    all_to_all x1, waiting for transfers between devices, on_device(): gathered = lax.all_to_all(gathered, 'kq', 0, 0)  6.27 us
    all_to_all x1, starting transfers between devices, on_device(): gathered = lax.all_to_all(gathered, 'kq', 0, 0)  4.67 us
    unnamed x11, local copies, waits for them, and re-layouts  2.04 us
    pallas_call x1, Pallas kernels, pack(): pl.pallas_call(pack_kernel, out_shape=jax.ShapeDtypeStruct((groups, 2 * f...  1.88 us
    reduce_sum x6, other arithmetic, dots(): total = jnp.sum(left * right, axis=(2, 3))  1.63 us
  transfers between devices with their start and end apart: 2, of which 2 were waited for; matrix products, arithmetic and copies ran while one was open for 3% of the time, Pallas kernels for 0%

profile of v7, /device:TPU:0, one launch (start us, length us, event | category | flops | bytes accessed | tf_op | source)
XLA Modules:
  0.0 56.2 jit_solution(11322680659370705118)
XLA Ops:
  0.6 1.9 %shard_map.95 = f32[16,5,8,256]{3,2,1,0:T(8,128)} custom-call(f32[16,2,8,256]{3,2,1,0:T(8,128)} %primary_ref.1, f32[16,2,8,256]{3,2,1,0:T(8,128)} %prior_ref.1, f32[8,256]{1,0:T(8,128)} %sigma_ref.1), custom_call_target="tpu_custom_call" | custom-call | tf_op jit(solution)/shard_map/pallas_call | solution.py:79
  2.5 7.4 %all-to-all-start = ((f32[16,5,8,256]{3,2,1,0:T(8,128)}), f32[16,5,8,256]{3,2,1,0:T(8,128)S(1)}, u32[]{:S(2)}, u32[]{:S(2)}) async-start(f32[16,5,8,256]{3,2,1,0:T(8,128)} %shard_map.95), calls=%async_computation | async-start | bytes 1310720 | tf_op jit(solution)/shard_map/all_to_all | solution.py:104
  9.9 0.6 %copy-done.2 = f32[16]{0:T(128)S(1)} copy-done((f32[16]{0:T(128)S(1)}, f32[16]{0:T(128)}, u32[]{:S(2)}) %copy-start.2) | copy-done | bytes 88
  10.6 0.6 %dynamic_slice.7 = f32[1]{0:T(128)} dynamic-slice(f32[16]{0:T(128)S(1)} %copy-done.2, s32[]{:T(128)S(6)} %select_n.15), dynamic_slice_sizes={1} | dynamic-slice | bytes 12 | tf_op jit(solution)/shard_map/dynamic_slice | solution.py:117
  12.5 0.6 %dynamic_slice.6 = f32[1]{0:T(128)} dynamic-slice(f32[16]{0:T(128)S(1)} %copy-done.3, s32[]{:T(128)S(6)} %select_n.15), dynamic_slice_sizes={1} | dynamic-slice | bytes 12 | tf_op jit(solution)/shard_map/dynamic_slice | solution.py:118
  13.2 0.7 %copy-done.1 = f32[2,32]{1,0:T(2,128)S(1)} copy-done((f32[2,32]{1,0:T(2,128)S(1)}, f32[2,32]{1,0:T(2,128)}, u32[]{:S(2)}) %copy-start.1) | copy-done | bytes 280
  13.9 0.7 %copy-done = s32[2,32]{1,0:T(2,128)S(1)} copy-done((s32[2,32]{1,0:T(2,128)S(1)}, s32[2,32]{1,0:T(2,128)}, u32[]{:S(2)}) %copy-start) | copy-done | bytes 280
  14.6 11.9 %all-to-all-done = f32[16,5,8,256]{3,2,1,0:T(8,128)S(1)} async-done(((f32[16,5,8,256]{3,2,1,0:T(8,128)}), f32[16,5,8,256]{3,2,1,0:T(8,128)S(1)}, u32[]{:S(2)}, u32[]{:S(2)}) %all-to-all-start) | async-done | bytes 655392 | tf_op jit(solution)/shard_map/all_to_all | solution.py:104
  27.3 0.2 fusion.67
  27.6 0.3 multiply_reduce_fusion.4
  28.0 0.2 multiply_reduce_fusion.3
  28.4 0.3 fusion.52
  28.9 0.7 %fusion.58 = f32[2,128]{1,0:T(2,128)S(1)} fusion(f32[1,2,128,256]{3,2,1,0:T(8,128)S(1)} %add_add_fusion, f32[]{:T(128)} %bitcast), kind=kLoop, calls=%fused_computation.89 | loop fusion | flops 256 | bytes 2052 | tf_op jit(solution)/shard_map/mul | solution.py:155
  29.6 0.6 %broadcast_in_dim.39 = f32[16,1,258]{2,1,0:T(1,128)} broadcast(f32[258]{0:T(512)S(1)} %pad_maximum_fusion), dimensions={2} | broadcast | bytes 17544 | tf_op jit(solution)/shard_map/broadcast_in_dim | solution.py:159
  30.2 4.7 %all-to-all-start.1 = ((f32[16,1,258]{2,1,0:T(1,128)}), f32[16,1,258]{2,1,0:T(1,128)S(1)}, u32[]{:S(2)}, u32[]{:S(2)}) async-start(f32[16,1,258]{2,1,0:T(1,128)} %broadcast_in_dim.39), calls=%async_computation.1 | async-start | bytes 49152 | tf_op jit(solution)/shard_map/all_to_all | solution.py:161
  35.2 6.3 %all-to-all-done.1 = f32[16,1,258]{2,1,0:T(1,128)S(1)} async-done(((f32[16,1,258]{2,1,0:T(1,128)}), f32[16,1,258]{2,1,0:T(1,128)S(1)}, u32[]{:S(2)}, u32[]{:S(2)}) %all-to-all-start.1) | async-done | bytes 16544 | tf_op jit(solution)/shard_map/all_to_all | solution.py:161
  41.8 0.6 %fusion.65 = (f32[2,32]{1,0:T(2,128)S(1)}, f32[2,32]{1,0:T(2,128)}) fusion(f32[2,32]{1,0:T(2,128)S(1)} %broadcast_subtract_fusion, f32[2,32]{1,0:T(2,128)S(1)} %multiply_reduce_fusion.9, f32[2,32]{1,0:T(2,128)S(1)} %multiply_reduce_fusion.8), kind=kLoop, calls=%fused_computation.118 | loop fusion | flops 128 | bytes 1280 | tf_op jit(solution)/shard_map/add | solution.py:174
  42.6 0.6 %broadcast_multiply_fusion.1 = f32[2,128]{1,0:T(2,128)S(1)} fusion(f32[2,128]{1,0:T(2,128)S(1)} %multiply_reduce_fusion.6, f32[]{:T(128)} %bitcast), kind=kLoop, calls=%fused_computation.115 | loop fusion | flops 256 | bytes 2052 | tf_op jit(solution)/shard_map/mul | solution.py:182
  43.3 0.2 fusion.31
  43.6 0.3 multiply_reduce_fusion.1
  43.9 0.2 multiply_reduce_fusion
  44.4 0.3 fusion.51
  45.1 10.5 %all_to_all.29 = f32[16,8,256]{2,1,0:T(8,128)S(1)} all-to-all(f32[16,8,256]{2,1,0:T(8,128)S(1)} %bitcast.30), channel_id=1, replica_groups=mesh['lines'=2,'col'=16] {'col'}, dimensions={0} | all-to-all | bytes 262144 | tf_op jit(solution)/shard_map/all_to_all | solution.py:197
  55.6 0.6 %reduce_sum.153 = f32[8,256]{1,0:T(8,128)} reduce(f32[16,8,256]{2,1,0:T(8,128)S(1)} %all_to_all.29, f32[]{:T(128)} %constant.13.clone.1), dimensions={0}, to_apply=%region_14.15 | reduce | flops 30720 | bytes 139268 | tf_op jit(solution)/shard_map/reduce_sum | solution.py:197
  (54 shorter events, 3.0 us)
Async XLA Ops:
  2.5 24.0 %all-to-all-start = ((f32[16,5,8,256]{3,2,1,0:T(8,128)}), f32[16,5,8,256]{3,2,1,0:T(8,128)S(1)}, u32[]{:S(2)}, u32[]{:S(2)}) async-start(f32[16,5,8,256]{3,2,1,0:T(8,128)} %shard_map.95), calls=%async_computation | async-start | bytes 1310720 | tf_op jit(solution)/shard_map/all_to_all | solution.py:104
  9.9 0.7 %copy-start.2 = (f32[16]{0:T(128)S(1)}, f32[16]{0:T(128)}, u32[]{:S(2)}) copy-start(f32[16]{0:T(128)} %param.10) | copy-start | bytes 196
  11.2 1.3 %copy-start.3 = (f32[16]{0:T(128)S(1)}, f32[16]{0:T(128)}, u32[]{:S(2)}) copy-start(f32[16]{0:T(128)} %param.11) | copy-start | bytes 196
  12.5 0.7 %copy-start.4 = (s32[2]{0:T(128)S(1)}, s32[2]{0:T(128)}, u32[]{:S(2)}) copy-start(s32[2]{0:T(128)} %param.12) | copy-start | bytes 28
  13.2 0.7 %copy-start.1 = (f32[2,32]{1,0:T(2,128)S(1)}, f32[2,32]{1,0:T(2,128)}, u32[]{:S(2)}) copy-start(f32[2,32]{1,0:T(2,128)} %param.14) | copy-start | bytes 772
  13.9 0.7 %copy-start = (s32[2,32]{1,0:T(2,128)S(1)}, s32[2,32]{1,0:T(2,128)}, u32[]{:S(2)}) copy-start(s32[2,32]{1,0:T(2,128)} %param.13) | copy-start | bytes 772
  30.2 11.2 %all-to-all-start.1 = ((f32[16,1,258]{2,1,0:T(1,128)}), f32[16,1,258]{2,1,0:T(1,128)S(1)}, u32[]{:S(2)}, u32[]{:S(2)}) async-start(f32[16,1,258]{2,1,0:T(1,128)} %broadcast_in_dim.39), calls=%async_computation.1 | async-start | bytes 49152 | tf_op jit(solution)/shard_map/all_to_all | solution.py:161

commit v8 on v7

--- a/solution.py
+++ b/solution.py
@@ -62,28 +62,29 @@
     return result + mass_scale * center * middle
 
 
-def pack_kernel(primary_ref, prior_ref, sigma_ref, send_ref):
+def pack_kernel(primary_ref, sigma_ref, send_ref):
     fields = primary_ref.shape[1]
     send_ref[:, 0:fields] = primary_ref[...]
-    send_ref[:, fields : 2 * fields] = prior_ref[...]
     sigma = sigma_ref[...]
     for target in range(send_ref.shape[0]):
-        send_ref[target, 2 * fields] = sigma
-
-
-def pack(primary, prior, sigma):
+        send_ref[target, fields] = sigma
+
+
+def pack(primary, sigma):
     groups, fields, rows, depth = primary.shape
     steps = 2 if groups % 2 == 0 else 1
     chunk = groups // steps
-    part = pl.BlockSpec((chunk, fields, rows, depth), lambda i: (i, 0, 0, 0))
     return pl.pallas_call(
         pack_kernel,
-        out_shape=jax.ShapeDtypeStruct((groups, 2 * fields + 1, rows, depth), jnp.float32),
+        out_shape=jax.ShapeDtypeStruct((groups, fields + 1, rows, depth), jnp.float32),
         grid=(steps,),
-        in_specs=[part, part, pl.BlockSpec((rows, depth), lambda i: (0, 0))],
-        out_specs=pl.BlockSpec((chunk, 2 * fields + 1, rows, depth), lambda i: (i, 0, 0, 0)),
+        in_specs=[
+            pl.BlockSpec((chunk, fields, rows, depth), lambda i: (i, 0, 0, 0)),
+            pl.BlockSpec((rows, depth), lambda i: (0, 0)),
+        ],
+        out_specs=pl.BlockSpec((chunk, fields + 1, rows, depth), lambda i: (i, 0, 0, 0)),
         interpret=INTERPRET,
-    )(primary, prior, sigma)
+    )(primary, sigma)
 
 def on_device(
     primary, conductivity, wavenumbers, quadrature, electrodes, far_pole, observed, prior_adjoint
@@ -99,14 +100,18 @@
     def by_group(array):
         return array.reshape(groups, fields, own_columns, depth)
 
-    send = pack(by_group(primary), by_group(prior_adjoint), conductivity)
+    send = pack(by_group(primary), conductivity)
     if groups > 1:
         send = lax.all_to_all(send, "kq", 0, 2, tiled=True)
     received = send[0]
     width = groups * own_columns
     primary = received[:fields].reshape(per_group, sources, width, depth)
-    prior_adjoint = received[fields : 2 * fields].reshape(per_group, sources, width, depth)
-    sigma = received[2 * fields]
+    sigma = received[fields]
+    chunk = fields * own_columns * depth
+    packet_size = sources * width + electrodes.shape[0]
+    prior_rows = jnp.concatenate(
+        [prior_adjoint.reshape(groups, chunk), jnp.zeros((groups, packet_size), jnp.float32)], axis=1
+    )
 
     columns = width * spread
     offset = block * width
@@ -156,9 +161,13 @@
     packet = jnp.concatenate([weighted.reshape(-1), electrodes.astype(jnp.float32)])
     pole_hits = (far_pole[:, :, None] == jnp.arange(far_pole.shape[1])[None, None, :]).astype(jnp.float32)
     packet, pole_hits, held = lax.optimization_barrier((packet, pole_hits, 0.0 - observed))
-    gathered = jnp.broadcast_to(packet[None], (groups,) + packet.shape)
+    outgoing = jnp.broadcast_to(packet[None], (groups,) + packet.shape)
+    outgoing = lax.dynamic_update_slice(prior_rows, outgoing, (0, chunk))
     if groups > 1:
-        gathered = lax.all_to_all(gathered, "kq", 0, 0)
+        outgoing = lax.all_to_all(outgoing, "kq", 0, 0)
+    prior_adjoint = outgoing[:, :chunk].reshape(groups, fields, own_columns, depth)
+    prior_adjoint = prior_adjoint.transpose(1, 0, 2, 3).reshape(per_group, sources, width, depth)
+    gathered = outgoing[:, chunk:]
     if spread > 1:
         gathered = lax.all_gather(gathered, "cs")
     gathered = gathered.reshape(spread * groups, -1)

time: 56.6 us -> 55.6 us (0.982)
  starting transfers between devices: 12.1 us -> 11.1 us
  waiting for transfers between devices: 18.2 us -> 17.5 us
    all_to_all x1, waiting for transfers between devices: 11.9 us -> 7.31 us  [on_device(): send = lax.all_to_all(send, 'kq', 0, 2, tiled=True)]
    all_to_all x1, waiting for transfers between devices: 6.27 us -> 10.2 us  [on_device(): outgoing = lax.all_to_all(outgoing, 'kq', 0, 0)]
    all_to_all x1, starting transfers between devices: 4.67 us -> 3.54 us  [on_device(): outgoing = lax.all_to_all(outgoing, 'kq', 0, 0)]
    all_to_all x0 -> x1, local copies, waits for them, and re-layouts: none -> 0.9 us  [on_device(): outgoing = lax.all_to_all(outgoing, 'kq', 0, 0)]
    broadcast_in_dim x1 -> x0, local copies, waits for them, and re-layouts: 0.62 us -> none  [on_device(): gathered = jnp.broadcast_to(packet[None], (groups,) + packet.shape)]
    unnamed x11 -> x15, local copies, waits for them, and re-layouts: 2.04 us -> 2.26 us
where the time goes in v8:
time: 55.6 us; the launch traced here: 55.2 us
  waiting for transfers between devices  17.5 us (31%)
  starting transfers between devices  11.1 us (20%)
  blocking collectives  10.7 us (19%)
  other arithmetic  6.08 us (11%)
  local copies, waits for them, and re-layouts  5.8 us (10%)
  between operations  2.29 us (4%)
  Pallas kernels  1.7 us (3%)
    all_to_all x1, blocking collectives, on_device(): gradient = jnp.sum(lax.all_to_all(gradient, 'kq', 0, 0, tiled=True), axis=0)  10.7 us
    all_to_all x1, waiting for transfers between devices, on_device(): outgoing = lax.all_to_all(outgoing, 'kq', 0, 0)  10.2 us
    all_to_all x1, starting transfers between devices, on_device(): send = lax.all_to_all(send, 'kq', 0, 2, tiled=True)  7.55 us
    all_to_all x1, waiting for transfers between devices, on_device(): send = lax.all_to_all(send, 'kq', 0, 2, tiled=True)  7.31 us
    all_to_all x1, starting transfers between devices, on_device(): outgoing = lax.all_to_all(outgoing, 'kq', 0, 0)  3.54 us
    unnamed x15, local copies, waits for them, and re-layouts  2.26 us
    pallas_call x1, Pallas kernels, pack(): pl.pallas_call(pack_kernel, out_shape=jax.ShapeDtypeStruct((groups, field...  1.7 us
    reduce_sum x6, other arithmetic, dots(): total = jnp.sum(left * right, axis=(2, 3))  1.63 us
  transfers between devices with their start and end apart: 2, of which 2 were waited for; matrix products, arithmetic and copies ran while one was open for 3% of the time, Pallas kernels for 0%

profile of v8, /device:TPU:0, one launch (start us, length us, event | category | flops | bytes accessed | tf_op | source)
XLA Modules:
  0.0 55.2 jit_solution(4295119285473685929)
XLA Ops:
  0.6 1.7 %shard_map.95 = f32[16,3,8,256]{3,2,1,0:T(8,128)} custom-call(f32[16,2,8,256]{3,2,1,0:T(8,128)} %primary_ref.1, f32[8,256]{1,0:T(8,128)} %sigma_ref.1), custom_call_target="tpu_custom_call" | custom-call | tf_op jit(solution)/shard_map/pallas_call | solution.py:77
  2.3 7.5 %all-to-all-start = ((f32[16,3,8,256]{3,2,1,0:T(8,128)}), f32[16,3,8,256]{3,2,1,0:T(8,128)S(1)}, u32[]{:S(2)}, u32[]{:S(2)}) async-start(f32[16,3,8,256]{3,2,1,0:T(8,128)} %shard_map.95), calls=%async_computation | async-start | bytes 786432 | tf_op jit(solution)/shard_map/all_to_all | solution.py:105
  9.9 0.6 %copy-done.3 = f32[16]{0:T(128)S(1)} copy-done((f32[16]{0:T(128)S(1)}, f32[16]{0:T(128)}, u32[]{:S(2)}) %copy-start.3) | copy-done | bytes 88
  10.5 0.6 %dynamic_slice.7 = f32[1]{0:T(128)} dynamic-slice(f32[16]{0:T(128)S(1)} %copy-done.3, s32[]{:T(128)S(6)} %select_n.15), dynamic_slice_sizes={1} | dynamic-slice | bytes 12 | tf_op jit(solution)/shard_map/dynamic_slice | solution.py:122
  12.5 0.7 %dynamic_slice.6 = f32[1]{0:T(128)} dynamic-slice(f32[16]{0:T(128)S(1)} %copy-done.4, s32[]{:T(128)S(6)} %select_n.15), dynamic_slice_sizes={1} | dynamic-slice | bytes 12 | tf_op jit(solution)/shard_map/dynamic_slice | solution.py:123
  13.3 0.7 %copy-done.2 = f32[2,32]{1,0:T(2,128)S(1)} copy-done((f32[2,32]{1,0:T(2,128)S(1)}, f32[2,32]{1,0:T(2,128)}, u32[]{:S(2)}) %copy-start.2) | copy-done | bytes 280
  14.0 0.7 %copy-done.1 = s32[2,32]{1,0:T(2,128)S(1)} copy-done((s32[2,32]{1,0:T(2,128)S(1)}, s32[2,32]{1,0:T(2,128)}, u32[]{:S(2)}) %copy-start.1) | copy-done | bytes 280
  14.7 7.3 %all-to-all-done = f32[16,3,8,256]{3,2,1,0:T(8,128)S(1)} async-done(((f32[16,3,8,256]{3,2,1,0:T(8,128)}), f32[16,3,8,256]{3,2,1,0:T(8,128)S(1)}, u32[]{:S(2)}, u32[]{:S(2)}) %all-to-all-start) | async-done | bytes 393248 | tf_op jit(solution)/shard_map/all_to_all | solution.py:105
  22.7 0.2 fusion.67
  23.1 0.3 multiply_reduce_fusion.4
  23.4 0.2 multiply_reduce_fusion.3
  23.9 0.3 fusion.52
  24.3 0.7 %fusion.58 = f32[2,128]{1,0:T(2,128)S(1)} fusion(f32[1,2,128,256]{3,2,1,0:T(8,128)S(1)} %add_add_fusion, f32[]{:T(128)} %bitcast), kind=kLoop, calls=%fused_computation.91 | loop fusion | flops 256 | bytes 2052 | tf_op jit(solution)/shard_map/mul | solution.py:160
  25.1 0.9 %all_to_all.25 = f32[16,1,4354]{2,1,0:T(1,128)} reshape(f32[16,4354]{1,0:T(8,128)S(1)} %pad_maximum_fusion) | data formatting | bytes 557312 | tf_op jit(solution)/shard_map/all_to_all | solution.py:167
  26.0 3.5 %all-to-all-start.1 = ((f32[16,1,4354]{2,1,0:T(1,128)}), f32[16,1,4354]{2,1,0:T(1,128)S(1)}, u32[]{:S(2)}, u32[]{:S(2)}) async-start(f32[16,1,4354]{2,1,0:T(1,128)} %all_to_all.25), calls=%async_computation.1 | async-start | bytes 573440 | tf_op jit(solution)/shard_map/all_to_all | solution.py:167
  29.7 10.2 %all-to-all-done.1 = f32[16,1,4354]{2,1,0:T(1,128)S(1)} async-done(((f32[16,1,4354]{2,1,0:T(1,128)}), f32[16,1,4354]{2,1,0:T(1,128)S(1)}, u32[]{:S(2)}, u32[]{:S(2)}) %all-to-all-start.1) | async-done | bytes 278688 | tf_op jit(solution)/shard_map/all_to_all | solution.py:167
  40.4 0.6 %fusion.65 = (f32[2,32]{1,0:T(2,128)S(1)}, f32[2,32]{1,0:T(2,128)}) fusion(f32[2,32]{1,0:T(2,128)S(1)} %broadcast_subtract_fusion, f32[2,32]{1,0:T(2,128)S(1)} %multiply_reduce_fusion.9, f32[2,32]{1,0:T(2,128)S(1)} %multiply_reduce_fusion.8), kind=kLoop, calls=%fused_computation.119 | loop fusion | flops 128 | bytes 1280 | tf_op jit(solution)/shard_map/add | solution.py:183
  41.1 0.6 %broadcast_multiply_fusion.1 = f32[2,128]{1,0:T(2,128)S(1)} fusion(f32[2,128]{1,0:T(2,128)S(1)} %multiply_reduce_fusion.6, f32[]{:T(128)} %bitcast), kind=kLoop, calls=%fused_computation.116 | loop fusion | flops 256 | bytes 2052 | tf_op jit(solution)/shard_map/mul | solution.py:191
  42.0 0.2 fusion.31
  42.4 0.3 multiply_reduce_fusion.1
  42.7 0.2 multiply_reduce_fusion
  43.1 0.3 fusion.51
  43.9 10.7 %all_to_all.32 = f32[16,8,256]{2,1,0:T(8,128)S(1)} all-to-all(f32[16,8,256]{2,1,0:T(8,128)S(1)} %bitcast.49), channel_id=1, replica_groups=mesh['lines'=2,'col'=16] {'col'}, dimensions={0} | all-to-all | bytes 262144 | tf_op jit(solution)/shard_map/all_to_all | solution.py:206
  54.5 0.6 %reduce_sum.153 = f32[8,256]{1,0:T(8,128)} reduce(f32[16,8,256]{2,1,0:T(8,128)S(1)} %all_to_all.32, f32[]{:T(128)} %constant.13.clone.1), dimensions={0}, to_apply=%region_14.15 | reduce | flops 30720 | bytes 139268 | tf_op jit(solution)/shard_map/reduce_sum | solution.py:206
  (61 shorter events, 3.2 us)
Async XLA Ops:
  2.3 10.8 %copy-start = (f32[16,2,8,256]{3,2,1,0:T(8,128)S(1)}, f32[16,2,8,256]{3,2,1,0:T(8,128)}, u32[]{:S(2)}) copy-start(f32[16,2,8,256]{3,2,1,0:T(8,128)} %param.15) | copy-start | bytes 786436
  2.3 19.7 %all-to-all-start = ((f32[16,3,8,256]{3,2,1,0:T(8,128)}), f32[16,3,8,256]{3,2,1,0:T(8,128)S(1)}, u32[]{:S(2)}, u32[]{:S(2)}) async-start(f32[16,3,8,256]{3,2,1,0:T(8,128)} %shard_map.95), calls=%async_computation | async-start | bytes 786432 | tf_op jit(solution)/shard_map/all_to_all | solution.py:105
  9.9 0.7 %copy-start.3 = (f32[16]{0:T(128)S(1)}, f32[16]{0:T(128)}, u32[]{:S(2)}) copy-start(f32[16]{0:T(128)} %param.10) | copy-start | bytes 196
  11.1 1.3 %copy-start.4 = (f32[16]{0:T(128)S(1)}, f32[16]{0:T(128)}, u32[]{:S(2)}) copy-start(f32[16]{0:T(128)} %param.11) | copy-start | bytes 196
  12.4 0.7 %copy-start.5 = (s32[2]{0:T(128)S(1)}, s32[2]{0:T(128)}, u32[]{:S(2)}) copy-start(s32[2]{0:T(128)} %param.12) | copy-start | bytes 28
  13.3 0.7 %copy-start.2 = (f32[2,32]{1,0:T(2,128)S(1)}, f32[2,32]{1,0:T(2,128)}, u32[]{:S(2)}) copy-start(f32[2,32]{1,0:T(2,128)} %param.14) | copy-start | bytes 772
  14.0 0.7 %copy-start.1 = (s32[2,32]{1,0:T(2,128)S(1)}, s32[2,32]{1,0:T(2,128)}, u32[]{:S(2)}) copy-start(s32[2,32]{1,0:T(2,128)} %param.13) | copy-start | bytes 772
  26.0 13.9 %all-to-all-start.1 = ((f32[16,1,4354]{2,1,0:T(1,128)}), f32[16,1,4354]{2,1,0:T(1,128)S(1)}, u32[]{:S(2)}, u32[]{:S(2)}) async-start(f32[16,1,4354]{2,1,0:T(1,128)} %all_to_all.25), calls=%async_computation.1 | async-start | bytes 573440 | tf_op jit(solution)/shard_map/all_to_all | solution.py:167

commit v9 on v8

--- a/solution.py
+++ b/solution.py
@@ -122,6 +122,8 @@
     own_waves = lax.dynamic_slice_in_dim(wavenumbers, group * per_group, per_group)
     weights = lax.dynamic_slice_in_dim(quadrature, group * per_group, per_group)
     mass_scale = (own_waves * own_waves)[:, None, None, None]
+    weight_rows = jnp.broadcast_to(weights[:, None, None], (per_group, sources, width))
+    prior_rows, weight_rows = lax.optimization_barrier((prior_rows, weight_rows))
     operator_faces = coefficients(wide_sigma[1:-1])
 
     def operate(state):
@@ -157,7 +159,7 @@
     total_field = primary + conjugate(source, None)
 
     surface = total_field[:, :, :, 0]
-    weighted = jnp.sum(weights[:, None, None] * surface, axis=0)
+    weighted = jnp.sum(weight_rows * surface, axis=0)
     packet = jnp.concatenate([weighted.reshape(-1), electrodes.astype(jnp.float32)])
     pole_hits = (far_pole[:, :, None] == jnp.arange(far_pole.shape[1])[None, None, :]).astype(jnp.float32)
     packet, pole_hits, held = lax.optimization_barrier((packet, pole_hits, 0.0 - observed))
@@ -188,7 +190,7 @@
     ).astype(jnp.float32)
     charge_cols = jnp.sum(charge[:, :, None] * own_picks[None], axis=1)
     surface_row = (jnp.arange(depth) == 0).astype(jnp.float32)
-    adjoint_source = weights[:, None, None, None] * charge_cols[None, :, :, None] * surface_row
+    adjoint_source = (weight_rows * charge_cols[None])[..., None] * surface_row
     adjoint = conjugate(adjoint_source, prior_adjoint)
 
     adjoint_next = next_column(adjoint, "cs")

time: 55.6 us -> 54 us (0.971)
  waiting for transfers between devices: 17.5 us -> 16 us
  other arithmetic: 6.08 us -> 4.72 us
  local copies, waits for them, and re-layouts: 5.8 us -> 7.16 us
    all_to_all x1, waiting for transfers between devices: 7.31 us -> 5.77 us  [on_device(): send = lax.all_to_all(send, 'kq', 0, 2, tiled=True)]
    mul x2 -> x1, other arithmetic: 1.35 us -> 0.01 us  [on_device(): adjoint_source = (weight_rows * charge_cols[None])[..., None] * surface_row]
    broadcast_in_dim x0 -> x1, local copies, waits for them, and re-layouts: none -> 0.65 us  [on_device(): jnp.broadcast_to(weights[:, None, None], (per_group, sources, width))]
    dynamic_update_slice x1, local copies, waits for them, and re-layouts: 0.01 us -> 0.63 us  [on_device(): outgoing = lax.dynamic_update_slice(prior_rows, outgoing, (0, chunk))]
  transfers between devices with their start and end apart: 2 -> 2, of which waited for: 2 -> 2; matrix products, arithmetic and copies ran while one was open for 3% -> 4% of each run, Pallas kernels for 0% -> 0%
where the time goes in v9:
time: 54 us; the launch traced here: 53.6 us
  waiting for transfers between devices  16 us (30%)
  starting transfers between devices  11.1 us (21%)
  blocking collectives  10.7 us (20%)
  local copies, waits for them, and re-layouts  7.16 us (13%)
  other arithmetic  4.72 us (9%)
  between operations  2.29 us (4%)
  Pallas kernels  1.7 us (3%)
    all_to_all x1, blocking collectives, on_device(): gradient = jnp.sum(lax.all_to_all(gradient, 'kq', 0, 0, tiled=True), axis=0)  10.7 us
    all_to_all x1, waiting for transfers between devices, on_device(): outgoing = lax.all_to_all(outgoing, 'kq', 0, 0)  10.2 us
    all_to_all x1, starting transfers between devices, on_device(): send = lax.all_to_all(send, 'kq', 0, 2, tiled=True)  7.55 us
    all_to_all x1, waiting for transfers between devices, on_device(): send = lax.all_to_all(send, 'kq', 0, 2, tiled=True)  5.77 us
    all_to_all x1, starting transfers between devices, on_device(): outgoing = lax.all_to_all(outgoing, 'kq', 0, 0)  3.54 us
    unnamed x15, local copies, waits for them, and re-layouts  2.27 us
    pallas_call x1, Pallas kernels, pack(): pl.pallas_call(pack_kernel, out_shape=jax.ShapeDtypeStruct((groups, field...  1.7 us
    reduce_sum x6, other arithmetic, dots(): total = jnp.sum(left * right, axis=(2, 3))  1.63 us
  transfers between devices with their start and end apart: 2, of which 2 were waited for; matrix products, arithmetic and copies ran while one was open for 4% of the time, Pallas kernels for 0%

profile of v9, /device:TPU:0, one launch (start us, length us, event | category | flops | bytes accessed | tf_op | source)
XLA Modules:
  0.0 53.6 jit_solution(13884901365913593658)
XLA Ops:
  0.6 1.7 %shard_map.95 = f32[16,3,8,256]{3,2,1,0:T(8,128)} custom-call(f32[16,2,8,256]{3,2,1,0:T(8,128)} %primary_ref.1, f32[8,256]{1,0:T(8,128)} %sigma_ref.1), custom_call_target="tpu_custom_call" | custom-call | tf_op jit(solution)/shard_map/pallas_call | solution.py:77
  2.3 7.5 %all-to-all-start = ((f32[16,3,8,256]{3,2,1,0:T(8,128)}), f32[16,3,8,256]{3,2,1,0:T(8,128)S(1)}, u32[]{:S(2)}, u32[]{:S(2)}) async-start(f32[16,3,8,256]{3,2,1,0:T(8,128)} %shard_map.95), calls=%async_computation | async-start | bytes 786432 | tf_op jit(solution)/shard_map/all_to_all | solution.py:105
  9.9 0.6 %copy-done.3 = f32[16]{0:T(128)S(1)} copy-done((f32[16]{0:T(128)S(1)}, f32[16]{0:T(128)}, u32[]{:S(2)}) %copy-start.3) | copy-done | bytes 88
  10.5 0.6 %dynamic_slice.7 = f32[1]{0:T(128)} dynamic-slice(f32[16]{0:T(128)S(1)} %copy-done.3, s32[]{:T(128)S(6)} %select_n.15), dynamic_slice_sizes={1} | dynamic-slice | bytes 12 | tf_op jit(solution)/shard_map/dynamic_slice | solution.py:122
  12.4 0.6 %dynamic_slice.6 = f32[1]{0:T(128)} dynamic-slice(f32[16]{0:T(128)S(1)} %copy-done.4, s32[]{:T(128)S(6)} %select_n.15), dynamic_slice_sizes={1} | dynamic-slice | bytes 12 | tf_op jit(solution)/shard_map/dynamic_slice | solution.py:123
  13.2 0.7 %broadcast_in_dim.39 = f32[1,2,128]{2,1,0:T(2,128)S(1)} broadcast(f32[]{:T(128)} %bitcast), dimensions={} | broadcast | bytes 1028 | tf_op jit(solution)/shard_map/broadcast_in_dim | solution.py:125
  13.9 0.9 %all_to_all.24 = f32[16,1,4354]{2,1,0:T(1,128)} reshape(f32[16,4354]{1,0:T(8,128)S(1)} %concatenate.117) | data formatting | bytes 557312 | tf_op jit(solution)/shard_map/all_to_all | solution.py:169
  14.9 0.7 %copy-done.2 = f32[2,32]{1,0:T(2,128)S(1)} copy-done((f32[2,32]{1,0:T(2,128)S(1)}, f32[2,32]{1,0:T(2,128)}, u32[]{:S(2)}) %copy-start.2) | copy-done | bytes 280
  15.5 0.7 %copy-done.1 = s32[2,32]{1,0:T(2,128)S(1)} copy-done((s32[2,32]{1,0:T(2,128)S(1)}, s32[2,32]{1,0:T(2,128)}, u32[]{:S(2)}) %copy-start.1) | copy-done | bytes 280
  16.3 5.8 %all-to-all-done = f32[16,3,8,256]{3,2,1,0:T(8,128)S(1)} async-done(((f32[16,3,8,256]{3,2,1,0:T(8,128)}), f32[16,3,8,256]{3,2,1,0:T(8,128)S(1)}, u32[]{:S(2)}, u32[]{:S(2)}) %all-to-all-start) | async-done | bytes 393248 | tf_op jit(solution)/shard_map/all_to_all | solution.py:105
  22.7 0.2 fusion.68
  23.1 0.3 multiply_reduce_fusion.4
  23.4 0.2 multiply_reduce_fusion.3
  23.9 0.3 fusion.52
  24.4 0.6 %broadcast_dynamic-update-slice_fusion = f32[16,1,4354]{2,1,0:T(1,128)} fusion(f32[16,1,4354]{2,1,0:T(1,128)} %all_to_all.24, f32[258]{0:T(512)S(1)} %pad_maximum_fusion), kind=kLoop, calls=%fused_computation.110 | loop fusion | bytes 25608 | tf_op jit(solution)/shard_map/dynamic_update_slice | solution.py:167
  25.1 3.5 %all-to-all-start.1 = ((f32[16,1,4354]{2,1,0:T(1,128)}), f32[16,1,4354]{2,1,0:T(1,128)S(1)}, u32[]{:S(2)}, u32[]{:S(2)}) async-start(f32[16,1,4354]{2,1,0:T(1,128)} %broadcast_dynamic-update-slice_fusion), calls=%async_computation.1 | async-start | bytes 573440 | tf_op jit(solution)/shard_map/all_to_all | solution.py:169
  28.8 10.2 %all-to-all-done.1 = f32[16,1,4354]{2,1,0:T(1,128)S(1)} async-done(((f32[16,1,4354]{2,1,0:T(1,128)}), f32[16,1,4354]{2,1,0:T(1,128)S(1)}, u32[]{:S(2)}, u32[]{:S(2)}) %all-to-all-start.1) | async-done | bytes 278688 | tf_op jit(solution)/shard_map/all_to_all | solution.py:169
  39.4 0.6 %fusion.66 = (f32[2,32]{1,0:T(2,128)S(1)}, f32[2,32]{1,0:T(2,128)}) fusion(f32[2,32]{1,0:T(2,128)S(1)} %broadcast_subtract_fusion, f32[2,32]{1,0:T(2,128)S(1)} %multiply_reduce_fusion.9, f32[2,32]{1,0:T(2,128)S(1)} %multiply_reduce_fusion.8), kind=kLoop, calls=%fused_computation.121 | loop fusion | flops 128 | bytes 1280 | tf_op jit(solution)/shard_map/add | solution.py:185
  40.5 0.2 fusion.31
  40.8 0.3 multiply_reduce_fusion.1
  41.1 0.2 multiply_reduce_fusion
  41.6 0.3 fusion.51
  42.3 10.7 %all_to_all.36 = f32[16,8,256]{2,1,0:T(8,128)S(1)} all-to-all(f32[16,8,256]{2,1,0:T(8,128)S(1)} %bitcast.60), channel_id=1, replica_groups=mesh['lines'=2,'col'=16] {'col'}, dimensions={0} | all-to-all | bytes 262144 | tf_op jit(solution)/shard_map/all_to_all | solution.py:208
  53.0 0.6 %reduce_sum.153 = f32[8,256]{1,0:T(8,128)} reduce(f32[16,8,256]{2,1,0:T(8,128)S(1)} %all_to_all.36, f32[]{:T(128)} %constant.9.clone.1), dimensions={0}, to_apply=%region_14.15 | reduce | flops 30720 | bytes 139268 | tf_op jit(solution)/shard_map/reduce_sum | solution.py:208
  (63 shorter events, 3.3 us)
Async XLA Ops:
  2.3 10.7 %copy-start = (f32[16,2,8,256]{3,2,1,0:T(8,128)S(1)}, f32[16,2,8,256]{3,2,1,0:T(8,128)}, u32[]{:S(2)}) copy-start(f32[16,2,8,256]{3,2,1,0:T(8,128)} %param.15) | copy-start | bytes 786436
  2.3 19.7 %all-to-all-start = ((f32[16,3,8,256]{3,2,1,0:T(8,128)}), f32[16,3,8,256]{3,2,1,0:T(8,128)S(1)}, u32[]{:S(2)}, u32[]{:S(2)}) async-start(f32[16,3,8,256]{3,2,1,0:T(8,128)} %shard_map.95), calls=%async_computation | async-start | bytes 786432 | tf_op jit(solution)/shard_map/all_to_all | solution.py:105
  9.9 0.7 %copy-start.3 = (f32[16]{0:T(128)S(1)}, f32[16]{0:T(128)}, u32[]{:S(2)}) copy-start(f32[16]{0:T(128)} %param.10) | copy-start | bytes 196
  11.1 1.3 %copy-start.4 = (f32[16]{0:T(128)S(1)}, f32[16]{0:T(128)}, u32[]{:S(2)}) copy-start(f32[16]{0:T(128)} %param.11) | copy-start | bytes 196
  13.2 0.7 %copy-start.5 = (s32[2]{0:T(128)S(1)}, s32[2]{0:T(128)}, u32[]{:S(2)}) copy-start(s32[2]{0:T(128)} %param.12) | copy-start | bytes 28
  14.8 0.7 %copy-start.2 = (f32[2,32]{1,0:T(2,128)S(1)}, f32[2,32]{1,0:T(2,128)}, u32[]{:S(2)}) copy-start(f32[2,32]{1,0:T(2,128)} %param.14) | copy-start | bytes 772
  15.5 0.7 %copy-start.1 = (s32[2,32]{1,0:T(2,128)S(1)}, s32[2,32]{1,0:T(2,128)}, u32[]{:S(2)}) copy-start(s32[2,32]{1,0:T(2,128)} %param.13) | copy-start | bytes 772
  25.1 13.9 %all-to-all-start.1 = ((f32[16,1,4354]{2,1,0:T(1,128)}), f32[16,1,4354]{2,1,0:T(1,128)S(1)}, u32[]{:S(2)}, u32[]{:S(2)}) async-start(f32[16,1,4354]{2,1,0:T(1,128)} %broadcast_dynamic-update-slice_fusion), calls=%async_computation.1 | async-start | bytes 573440 | tf_op jit(solution)/shard_map/all_to_all | solution.py:169
